TPU v7x, 256 devices: a whole 4x4x8 slice. The times are simulated.
256 devices in a mesh: lat: 8 (over x, y_hi), lon: 8 (over z), lev: 4 (over y_lo, core).
Axes of the slice: x: 4, y: 4 (y_hi: 2, y_lo: 2; y = y_hi * 2 + y_lo), z: 8, core: 2. Of those that a mesh axis runs over, the one named last changes fastest.
Arguments:
- fields: float32 [3, 16, 1280, 3072], P(None, 'lev', 'lat', 'lon'), may hold values from -6 to 6
- sl_weights: float32 [40, 24, 128, 128], P('lat', 'lon'), may hold values from -0.5 to 0.5
- sl_tile: int32 [40, 24], P('lat', 'lon'), may hold values from -1 to 1
- daylit: int32 [1280, 24], P('lat', 'lon'), may hold values from 0 to 1, as said below
- absorption: float32 [32], replicated, may hold values from 0.05 to 5
- continuum: float32 [32], replicated, may hold values from 0.05 to 2
- albedo: float32 [32], replicated, may hold values from 0.5 to 0.95
- wave_ids: int32 [640], replicated, may hold values from 0 to 639, each once
- legendre: float32 [640, 640, 1280], P(('lat', 'lon'), 'lev'), may hold values from -0.15625 to 0.15625
Outputs:
- spectral: float32 [640, 2, 3, 16, 640], P(('lat', 'lon'), None, None, None, 'lev')
Inputs may be any that keep to these rules, and one draw needn't show every extreme that they name: `daylit`: in every latitude row, at most one of the blocks b and b + 12 is sunlit. `wave_ids`: every wavenumber appears in exactly one slot.
All inputs are finite; a program needn't handle non-finite values.
Results may differ from a plain program's by a relative error of at most 0.000068.
Values sent between devices are 32-bit elements; how exact they have to be, the bound alone decides.
No kernel may reach another device: no remote copies, remote signals or barrier semaphores. Data moves between devices by JAX's collectives and lax.ppermute only.
A program may use at most 192 MiB of HBM per device.

v0:
```python
import math

import jax
import jax.numpy as jnp
from jax import lax
from jax.sharding import PartitionSpec as P

highest = lax.Precision.HIGHEST
heat_rate = 6.0
asymmetry = 0.6


def with_halo(block, sides, width):
    for axis, dim in sides:
        count = lax.axis_size(axis)
        forward = [(i, i + 1) for i in range(count - 1)]
        forward.append((count - 1, 0))
        backward = [(target, source) for source, target in forward]
        low = lax.ppermute(
            lax.slice_in_dim(block, block.shape[dim] - width, None, axis=dim), axis, forward
        )
        high = lax.ppermute(lax.slice_in_dim(block, 0, width, axis=dim), axis, backward)
        block = jnp.concatenate([low, block, high], axis=dim)
    return block


def carried_in(planes, axis):
    mine = lax.axis_index(axis)
    pieces = lax.all_gather(planes, axis)
    count = pieces.shape[0]
    below = (jnp.arange(count, dtype=jnp.int32) < mine).reshape((count,) + (1,) * planes.ndim)
    return jnp.sum(jnp.where(below, pieces, 0.0), axis=0)


def absorbed_per_band(
    depth_wet,
    hot_extinction_thickness,
    above_wet,
    above_warm,
    absorb_part,
    continuum_part,
    reflectivity_share,
):
    gamma_one = (7.0 - reflectivity_share * (4.0 + 3.0 * asymmetry)) / 4.0
    gamma_two = -(1.0 - reflectivity_share * (4.0 - 3.0 * asymmetry)) / 4.0
    eigen_rate = jnp.sqrt(gamma_one * gamma_one - gamma_two * gamma_two)
    optical = absorb_part * depth_wet + continuum_part * hot_extinction_thickness
    beam = jnp.exp(-(absorb_part * above_wet + continuum_part * above_warm))
    decay = jnp.exp(-eigen_rate * optical)
    decay_sq = decay * decay
    denominator = eigen_rate + gamma_one + (eigen_rate - gamma_one) * decay_sq
    lost = (gamma_two * (1.0 - decay_sq) + 2.0 * eigen_rate * decay) / denominator
    return beam * (1.0 - lost)


def absorbed_mean(
    depth_wet, hot_extinction_thickness, above_wet, above_warm, absorption, continuum, albedo
):
    band_total = absorption.shape[0]
    band_group = min(8, band_total)
    unit_shape = (1,) * depth_wet.ndim
    running = jnp.zeros_like(depth_wet)
    for band_start in range(0, band_total, band_group):
        absorb_part = absorption[band_start : band_start + band_group].reshape(
            (band_group,) + unit_shape
        )
        continuum_part = continuum[band_start : band_start + band_group].reshape(
            (band_group,) + unit_shape
        )
        reflectivity_share = albedo[band_start : band_start + band_group].reshape(
            (band_group,) + unit_shape
        )
        terms = absorbed_per_band(
            depth_wet[None],
            hot_extinction_thickness[None],
            above_wet[None],
            above_warm[None],
            absorb_part,
            continuum_part,
            reflectivity_share,
        )
        running = running + jnp.sum(terms, axis=0)
    return running / band_total


def local(fields, sl_weights, sl_tile, daylit, absorption, continuum, albedo, wave_ids, legendre):
    meridian_number = lax.axis_size("lon")
    lat_count = lax.axis_size("lat")
    lev_count = lax.axis_size("lev")
    wave_devices = lat_count * meridian_number
    field_count, lev_local, lat_local, lon_local = fields.shape
    tile_width = sl_weights.shape[-1]
    tile_count = lon_local // tile_width
    row_blocks = sl_tile.shape[0]
    block_rows = lat_local // row_blocks
    padded = with_halo(fields, (("lon", 3),), tile_width)
    source_ids = jnp.arange(tile_count, dtype=jnp.int32)[None, :] + 1 + sl_tile
    onehot = (
        source_ids[:, :, None] == jnp.arange(tile_count + 2, dtype=jnp.int32)[None, None, :]
    ).astype(jnp.float32)
    blocks = (sl_weights[:, :, :, None, :] * onehot[:, :, None, :, None]).reshape(
        row_blocks, lon_local, (tile_count + 2) * tile_width
    )
    padded_rows = padded.reshape(field_count, lev_local, row_blocks, block_rows, -1)
    departure_estimate = jnp.einsum(
        "flbrk,bnk->bflrn", padded_rows, blocks, precision=highest
    )
    departure_estimate = departure_estimate.transpose(1, 2, 0, 3, 4).reshape(
        field_count, lev_local, lat_local, lon_local
    )
    moisture = departure_estimate[2]
    thermal_state = departure_estimate[0]
    stratum_factor = 4.0 / (lev_local * lev_count)
    depth_wet = stratum_factor * (0.2 + moisture * moisture)
    hot_extinction_thickness = stratum_factor * (0.2 + thermal_state * thermal_state)
    prefix = carried_in(
        jnp.stack([jnp.sum(depth_wet, axis=0), jnp.sum(hot_extinction_thickness, axis=0)]), "lev"
    )
    prefix_wet, prefix_warm = prefix[0], prefix[1]
    wet_levels = []
    warm_levels = []
    for level in range(lev_local):
        wet_levels.append(prefix_wet)
        warm_levels.append(prefix_warm)
        prefix_wet = prefix_wet + depth_wet[level]
        prefix_warm = prefix_warm + hot_extinction_thickness[level]
    above_wet = jnp.stack(wet_levels, axis=0)
    above_warm = jnp.stack(warm_levels, axis=0)
    absorbed = absorbed_mean(
        depth_wet, hot_extinction_thickness, above_wet, above_warm, absorption, continuum, albedo
    )
    absorbed = absorbed.reshape(lev_local, lat_local, tile_count, tile_width)
    heating = (absorbed * daylit.astype(jnp.float32)[None, :, :, None]).reshape(
        lev_local, lat_local, lon_local
    )
    chunk_rows = lev_local * lat_local // meridian_number
    halves = lat_local // chunk_rows

    def to_sectors(block):
        lines = block.reshape(block.shape[0], meridian_number, chunk_rows, lon_local)
        return lax.all_to_all(lines, "lon", split_axis=1, concat_axis=1, tiled=True)

    sectors_rest = to_sectors(departure_estimate[1:])
    sectors_heat = to_sectors(departure_estimate[:1] + heat_rate * heating[None])
    lon_total = lon_local * meridian_number
    wave_total = wave_ids.shape[0]
    inner = jnp.arange(lon_local, dtype=jnp.int32)
    phases = wave_ids[:, None] * inner[None, :] % lon_total
    angles = phases.astype(jnp.float32) * (2.0 * math.pi / lon_total)
    scale = 1.0 / math.sqrt(lon_total)
    dft_table = jnp.concatenate([jnp.cos(angles) * scale, jnp.sin(angles) * scale], axis=0)
    turns = wave_ids[None, :] * jnp.arange(meridian_number, dtype=jnp.int32)[:, None] % meridian_number
    turn_angles = turns.astype(jnp.float32) * (2.0 * math.pi / meridian_number)
    turn_cos = jnp.cos(turn_angles)[:, None, :]
    turn_sin = jnp.sin(turn_angles)[:, None, :]

    def transform(sectors):
        partial = jnp.einsum("fdqn,wn->fdqw", sectors, dft_table, precision=highest)
        cos_part = partial[..., :wave_total]
        sin_part = partial[..., wave_total:]
        real_part = jnp.sum(turn_cos * cos_part - turn_sin * sin_part, axis=1)
        imag_part = -jnp.sum(turn_sin * cos_part + turn_cos * sin_part, axis=1)
        return jnp.stack([real_part, imag_part], axis=1)

    fourier = jnp.concatenate([transform(sectors_heat), transform(sectors_rest)], axis=0)
    waves_local = wave_total // wave_devices
    outgoing_waves = (
        fourier.reshape(field_count, 2, chunk_rows, wave_devices, waves_local)
        .transpose(3, 1, 4, 0, 2)
        .reshape(wave_devices, 2 * waves_local, field_count * chunk_rows)
    )
    arrived = lax.all_to_all(
        outgoing_waves, ("lat", "lon"), split_axis=0, concat_axis=0, tiled=True
    )
    arrived = arrived.reshape(
        lat_count, lev_local, halves, 2, waves_local, field_count, chunk_rows
    )
    spectral_in = arrived.transpose(4, 3, 5, 1, 0, 2, 6).reshape(
        waves_local, 2, field_count, lev_local, lat_count * lat_local
    )
    spectra = jnp.einsum(
        "mcfls,mns->mcfln",
        lax.all_gather(spectral_in, "lev", axis=3, tiled=True),
        legendre,
        precision=highest,
    )
    degree_local = legendre.shape[1]
    degrees = lax.axis_index("lev") * degree_local + jnp.arange(degree_local, dtype=jnp.int32)
    own_waves = lax.dynamic_slice_in_dim(
        wave_ids, lax.axis_index(("lat", "lon")) * waves_local, waves_local
    )
    keep_mask = degrees[None, :] >= own_waves[:, None]
    return jnp.where(keep_mask[:, None, None, None, :], spectra, 0.0)


def solution(mesh):
    in_specs = (
        P(None, "lev", "lat", "lon"),
        P("lat", "lon", None, None),
        P("lat", "lon"),
        P("lat", "lon"),
        P(),
        P(),
        P(),
        P(),
        P(("lat", "lon"), "lev", None),
    )
    out_specs = P(("lat", "lon"), None, None, None, "lev")
    return jax.shard_map(local, mesh=mesh, in_specs=in_specs, out_specs=out_specs, check_vma=False)
```

profile of v0, /device:TPU:1, one launch (start us, length us, event | category | flops | bytes accessed | tf_op | source)
XLA Modules:
  0.0 296.4 jit_solution(16400914566595285234)
XLA Ops:
  6.5 3.0 fusion.55
  9.5 6.4 %collective-permute-start.1 = (f32[3,4,160,128]{3,2,1,0:T(8,128)}, f32[3,4,160,128]{3,2,1,0:T(8,128)}, u32[]{:S(2)}, u32[]{:S(2)}) collective-permute-start(f32[3,4,160,128]{3,2,1,0:T(8,128)} %get-tuple-element.37), channel_id=1, source_target_pairs={{4,0},{8,4},{12,8},{16,12},{20,16},{24,20},{28,24},{0,28},{5,1},{9... | collective-permute-start | bytes 2949128 | tf_op jit(solution)/shard_map/ppermute | solution.py:22
  15.9 0.8 broadcast_add_fusion
  16.8 2.4 copy.62
  19.2 5.7 %broadcast_multiply_fusion = f32[5,3,128,5,128]{2,1,4,3,0:T(4,128)} fusion(f32[5,3,5]{1,2,0:T(8,128)S(1)} %fusion.34, f32[5,3,128,128]{2,1,3,0:T(4,128)} %copy.62), kind=kLoop, calls=%fused_computation.14 | loop fusion | flops 1228800 | bytes 5898540 | tf_op jit(solution)/shard_map/mul | solution.py:101
  24.9 9.0 %mul.624 = f32[5,384,640]{1,2,0:T(8,128)} reshape(f32[5,3,128,5,128]{2,1,4,3,0:T(4,128)} %broadcast_multiply_fusion) | data formatting | bytes 9830400 | tf_op jit(solution)/shard_map/mul | solution.py:101
  33.9 2.7 collective-permute-done.1
  36.6 3.1 %collective-permute-done = f32[3,4,160,128]{3,2,1,0:T(8,128)} collective-permute-done((f32[3,4,160,128]{3,2,1,0:T(8,128)}, f32[3,4,160,128]{3,2,1,0:T(8,128)}, u32[]{:S(2)}, u32[]{:S(2)}) %collective-permute-start) | collective-permute-done | bytes 983072 | tf_op jit(solution)/shard_map/ppermute | solution.py:19
  39.7 1.9 pad_maximum_fusion
  41.7 9.0 %fusion.10 = f32[3,4,5,32,384]{4,3,1,0,2:T(8,128)S(1)} fusion(f32[5,384,640]{1,2,0:T(8,128)S(1)} %copy-done, f32[3,4,5,32,640]{4,3,2,1,0:T(8,128)S(1)} %bitcast.68), kind=kOutput, calls=%fused_computation.21 | convolution fusion | flops 5662310400 | bytes 12779520 | tf_op jit(solution)/shard_map/flbrk,bnk->bflrn/dot_general | solution.py:105
  50.6 1.8 fusion.48
  52.4 0.8 pad_maximum_fusion.6
  53.4 0.2 broadcast.256
  53.7 0.5 iota_compare_fusion.1
  54.6 0.1 slice.159
  54.7 0.1 copy.71
  54.9 1.5 copy.72
  56.3 3.8 %all-to-all-start.1 = ((f32[2,8,80,384]{3,2,0,1:T(8,128)}), f32[2,8,80,384]{3,2,0,1:T(8,128)S(1)}, u32[]{:S(2)}, u32[]{:S(2)}) async-start(f32[2,8,80,384]{3,2,0,1:T(8,128)} %copy.72), calls=%async_computation.1 | async-start | bytes 3932160 | tf_op jit(solution)/shard_map/all_to_all | solution.py:141
  60.1 2.2 copy.66
  62.4 1.0 copy.68
  63.4 2.3 copy.67
  65.7 2.3 fusion.56
  68.0 15.3 %all-gather.6.cloned.1.call-done = f32[8,160,384]{2,1,0:T(8,128)} async-done(((f32[2,160,384]{2,1,0:T(8,128)}), f32[8,160,384]{2,1,0:T(8,128)}) %all-gather.6.cloned.1.call-update) | async-done | bytes 1966096 | tf_op jit(solution)/shard_map/all_gather | solution.py:29
  83.2 1.9 select_reduce_fusion
  85.1 1.5 fusion.52
  86.8 13.2 %multiply_reduce_fusion.3 = (f32[4,160,384]{2,1,0:T(8,128)S(1)}, f32[4,160,384]{2,1,0:T(8,128)S(1)}) fusion(f32[8]{0:T(128)S(1)} %get-tuple-element.73, f32[8]{0:T(128)S(1)} %get-tuple-element.74, f32[8]{0:T(128)S(1)} %get-tuple-element.75, f32[4,160,384]{2,1,0:T(8,128)S(1)} %bitcast.77, f32[4,160,384]{2,1,0:T(8,128)S(1)} %bitcast.79, ...), kind=kLoop, calls=%fused_computation.5 | loop fusion | flops 74219520 | bytes 5898688 | tf_op jit(solution)/shard_map/reduce_sum | solution.py:82
  100.0 13.2 %multiply_reduce_fusion.2 = (f32[4,160,384]{2,1,0:T(8,128)S(1)}, f32[4,160,384]{2,1,0:T(8,128)S(1)}) fusion(f32[8]{0:T(128)S(1)} %get-tuple-element.70, f32[8]{0:T(128)S(1)} %get-tuple-element.71, f32[8]{0:T(128)S(1)} %get-tuple-element.72, f32[8]{0:T(128)S(1)} %get-tuple-element.82, f32[8]{0:T(128)S(1)} %get-tuple-element.84, f32[8]{0:T(128)S(1)} %get-tuple-element.66, ...), kind=kLoop, calls=%fused_computation.4 | loop fusion | flops 74219520 | bytes 5898688 | tf_op jit(solution)/shard_map/reduce_sum | solution.py:82
  113.2 0.2 multiply_multiply_fusion
  113.5 1.0 add_bitcast_fusion
  114.5 6.7 %all-to-all-start = ((f32[1,8,80,384]{3,2,0,1:T(8,128)}), f32[1,8,80,384]{3,2,0,1:T(8,128)S(1)}, u32[]{:S(2)}, u32[]{:S(2)}) async-start(f32[1,8,80,384]{3,2,0,1:T(8,128)} %add_bitcast_fusion), calls=%async_computation | async-start | bytes 1966080 | tf_op jit(solution)/shard_map/all_to_all | solution.py:141
  121.2 0.4 all-gather.4.cloned.1.call-start
  121.8 4.1 %cosine_multiply_fusion = (f32[640,384]{1,0:T(8,128)S(1)}, f32[640,384]{1,0:T(8,128)S(1)}) fusion(s32[640]{0:T(1024)S(1)} %copy-done.9), kind=kLoop, calls=%fused_computation.37 | loop fusion | flops 2703360 | bytes 1968640 | tf_op jit(solution)/shard_map/mul | solution.py:151
  125.9 12.2 %fusion.6 = f32[2,8,80,1280]{3,2,1,0:T(8,128)S(1)} fusion(f32[2,8,80,384]{3,2,0,1:T(8,128)} %copy-done.2, f32[640,384]{1,0:T(8,128)S(1)} %get-tuple-element.52, f32[640,384]{1,0:T(8,128)S(1)} %get-tuple-element.51), kind=kOutput, calls=%fused_computation.16 | convolution fusion | flops 7550238720 | bytes 10485760 | tf_op jit(solution)/shard_map/fdqn,wn->fdqw/dot_general | solution.py:158
  138.1 1.7 subtract_reduce_fusion
  139.8 9.3 %all-to-all-done = f32[1,8,80,384]{3,2,0,1:T(8,128)S(1)} async-done(((f32[1,8,80,384]{3,2,0,1:T(8,128)}), f32[1,8,80,384]{3,2,0,1:T(8,128)S(1)}, u32[]{:S(2)}, u32[]{:S(2)}) %all-to-all-start) | async-done | bytes 983072 | tf_op jit(solution)/shard_map/all_to_all | solution.py:141
  149.1 5.6 %convolution_bitcast_fusion = f32[1,8,80,1280]{3,2,1,0:T(8,128)S(1)} fusion(f32[640,384]{1,0:T(8,128)S(1)} %get-tuple-element.52, f32[640,384]{1,0:T(8,128)S(1)} %get-tuple-element.51, f32[1,8,80,384]{3,2,0,1:T(8,128)S(1)} %all-to-all-done), kind=kOutput, calls=%fused_computation.11 | convolution fusion | flops 3775365120 | bytes 6225920 | tf_op jit(solution)/shard_map/fdqn,wn->fdqw/dot_general | solution.py:158
  154.7 0.5 subtract_reduce_fusion.1
  155.2 0.1 maximum_maximum_fusion
  155.3 2.5 copy.75
  157.8 2.9 copy.87
  160.7 2.0 reshape.369
  162.7 45.8 %all_to_all.15 = f32[64,20,240]{2,1,0:T(8,128)S(1)} all-to-all(f32[64,20,240]{2,1,0:T(8,128)} %reshape.369), channel_id=1, replica_groups=mesh['lat'=8,'lon'=8,'lev'=4] {'lat','lon'}, dimensions={0} | all-to-all | bytes 2457600 | tf_op jit(solution)/shard_map/all_to_all | solution.py:172
  208.5 1.5 copy.78
  210.0 2.9 reshape.357
  212.9 2.4 copy.88
  215.3 6.2 %reshape.370 = f32[10,2,3,4,1280]{4,1,2,0,3:T(2,128)} reshape(f32[10,2,3,4,8,2,80]{6,5,4,1,2,0,3:T(2,128)} %copy.88) | data formatting | bytes 2457600 | tf_op jit(solution)/shard_map/reshape | solution.py:178
  221.7 53.3 %all-gather.4.cloned.1.call-done = f32[10,2,3,16,1280]{4,1,2,0,3:T(2,128)} async-done(((f32[10,2,3,4,1280]{4,1,2,0,3:T(2,128)}), f32[10,2,3,16,1280]{4,1,2,0,3:T(2,128)}) %all-gather.4.cloned.1.call-update) | async-done | bytes 4915216 | tf_op jit(solution)/shard_map/all_gather | solution.py:183
  275.0 14.3 %fusion.15 = f32[10,2,3,16,160]{4,3,2,1,0:T(8,128)} fusion(f32[10,160,1280]{2,1,0:T(8,128)} %param.17, f32[10,2,3,16,1280]{4,1,2,0,3:T(2,128)} %all-gather.4.cloned.1.call-done, pred[10,160]{1,0:T(8,128)(4,1)S(1)} %broadcast_compare_fusion), kind=kOutput, calls=%fused_computation.25 | convolution fusion | flops 2359449600 | bytes 13723200 | tf_op jit(solution)/shard_map/mcfls,mns->mcfln/dot_general | solution.py:181
  (50 shorter events, 1.1 us)
Async XLA Ops:
  6.5 76.7 %all-gather.6.cloned.1.call-start = ((), (), s32[]{:S(2)}) async-start(), calls=%async_computation.4 | async-start | bytes 2457600 | tf_op jit(solution)/shard_map/all_gather | solution.py:29
  9.5 27.1 %collective-permute-start.1 = (f32[3,4,160,128]{3,2,1,0:T(8,128)}, f32[3,4,160,128]{3,2,1,0:T(8,128)}, u32[]{:S(2)}, u32[]{:S(2)}) collective-permute-start(f32[3,4,160,128]{3,2,1,0:T(8,128)} %get-tuple-element.37), channel_id=1, source_target_pairs={{4,0},{8,4},{12,8},{16,12},{20,16},{24,20},{28,24},{0,28},{5,1},{9... | collective-permute-start | bytes 2949128 | tf_op jit(solution)/shard_map/ppermute | solution.py:22
  15.9 23.8 %collective-permute-start = (f32[3,4,160,128]{3,2,1,0:T(8,128)}, f32[3,4,160,128]{3,2,1,0:T(8,128)}, u32[]{:S(2)}, u32[]{:S(2)}) collective-permute-start(f32[3,4,160,128]{3,2,1,0:T(8,128)} %get-tuple-element.36), channel_id=1, source_target_pairs={{0,4},{4,8},{8,12},{12,16},{16,20},{20,24},{24,28},{28,0},{1,5},{5... | collective-permute-start | bytes 2949128 | tf_op jit(solution)/shard_map/ppermute | solution.py:19
  19.2 20.6 %copy-start.1 = (f32[3,4,160,384]{3,2,1,0:T(8,128)S(1)}, f32[3,4,160,384]{3,2,1,0:T(8,128)}, u32[]{:S(2)}) copy-start(f32[3,4,160,384]{3,2,1,0:T(8,128)} %param.9) | copy-start | bytes 8847364
  33.9 7.7 %copy-start = (f32[5,384,640]{1,2,0:T(8,128)S(1)}, f32[5,384,640]{1,2,0:T(8,128)}, u32[]{:S(2)}) copy-start(f32[5,384,640]{1,2,0:T(8,128)} %mul.624) | copy-start | bytes 14745604
  41.6 11.7 %copy-start.12 = (s32[160,3]{0,1:T(4,128)S(1)}, s32[160,3]{0,1:T(4,128)}, u32[]{:S(2)}) copy-start(s32[160,3]{0,1:T(4,128)} %param.12) | copy-start | bytes 5764
  41.6 12.6 %copy-start.11 = (f32[32]{0:T(128)S(1)}, f32[32]{0:T(128)}, u32[]{:S(2)}) copy-start(f32[32]{0:T(128)} %param.14) | copy-start | bytes 388
  41.6 12.7 %copy-start.8 = (f32[32]{0:T(128)S(1)}, f32[32]{0:T(128)}, u32[]{:S(2)}) copy-start(f32[32]{0:T(128)} %param.15) | copy-start | bytes 388
  41.7 12.7 %copy-start.10 = (f32[32]{0:T(128)S(1)}, f32[32]{0:T(128)}, u32[]{:S(2)}) copy-start(f32[32]{0:T(128)} %param.13) | copy-start | bytes 388
  54.7 7.7 %copy-start.3 = (f32[1,4,5,32,384]{4,3,1,0,2:T(8,128)S(1)}, f32[1,4,5,32,384]{4,3,1,0,2:T(8,128)}, u32[]{:S(2)}) copy-start(f32[1,4,5,32,384]{4,3,1,0,2:T(8,128)} %get-tuple-element.33) | copy-start | bytes 2949124
  56.3 58.2 %all-to-all-start.1 = ((f32[2,8,80,384]{3,2,0,1:T(8,128)}), f32[2,8,80,384]{3,2,0,1:T(8,128)S(1)}, u32[]{:S(2)}, u32[]{:S(2)}) async-start(f32[2,8,80,384]{3,2,0,1:T(8,128)} %copy.72), calls=%async_computation.1 | async-start | bytes 3932160 | tf_op jit(solution)/shard_map/all_to_all | solution.py:141
  68.0 18.8 %copy-start.6 = (f32[1,4,5,32,384]{4,3,2,1,0:T(8,128)S(1)}, f32[1,4,5,32,384]{4,3,2,1,0:T(8,128)}, u32[]{:S(2)}) copy-start(f32[1,4,5,32,384]{4,3,2,1,0:T(8,128)} %copy.68) | copy-start | bytes 2949124
  83.2 3.6 %copy-start.7 = (f32[1,4,5,32,384]{4,3,2,1,0:T(8,128)S(1)}, f32[1,4,5,32,384]{4,3,2,1,0:T(8,128)}, u32[]{:S(2)}) copy-start(f32[1,4,5,32,384]{4,3,2,1,0:T(8,128)} %copy.67) | copy-start | bytes 2949124
  100.0 13.4 %copy-start.4 = (f32[1,4,5,32,384]{4,3,2,1,0:T(8,128)S(1)}, f32[1,4,5,32,384]{4,3,2,1,0:T(8,128)}, u32[]{:S(2)}) copy-start(f32[1,4,5,32,384]{4,3,2,1,0:T(8,128)} %copy.66) | copy-start | bytes 2949124
  113.2 8.5 %copy-start.9 = (s32[640]{0:T(1024)S(1)}, s32[640]{0:T(1024)}, u32[]{:S(2)}) copy-start(s32[640]{0:T(1024)} %param.16) | copy-start | bytes 7684
  114.5 7.2 %copy-start.2 = (f32[2,8,80,384]{3,2,0,1:T(8,128)}, f32[2,8,80,384]{3,2,0,1:T(8,128)S(1)}, u32[]{:S(2)}) copy-start(f32[2,8,80,384]{3,2,0,1:T(8,128)S(1)} %all-to-all-done.1) | copy-start | bytes 5898244
  114.5 34.6 %all-to-all-start = ((f32[1,8,80,384]{3,2,0,1:T(8,128)}), f32[1,8,80,384]{3,2,0,1:T(8,128)S(1)}, u32[]{:S(2)}, u32[]{:S(2)}) async-start(f32[1,8,80,384]{3,2,0,1:T(8,128)} %add_bitcast_fusion), calls=%async_computation | async-start | bytes 1966080 | tf_op jit(solution)/shard_map/all_to_all | solution.py:141
  121.2 153.8 %all-gather.4.cloned.1.call-start = ((), (), s32[]{:S(2)}) async-start(), calls=%async_computation.3 | async-start | bytes 6144000 | tf_op jit(solution)/shard_map/all_gather | solution.py:183
  149.1 6.1 %copy-start.5 = (f32[2,80,640]{2,1,0:T(8,128)S(1)}, f32[2,80,640]{2,1,0:T(8,128)}, u32[]{:S(2)}) copy-start(f32[2,80,640]{2,1,0:T(8,128)} %get-tuple-element.5) | copy-start | bytes 1228804
Sparse Core Ops, SparseCore 0:
  53.4 29.7 all-gather.5
  221.6 53.3 all-gather.3
where the time goes:
time: 300 us; the launch traced here: 296 us
  waiting for transfers between devices  83.7 us (28%)
  other arithmetic  49.5 us (16%)
  blocking collectives  45.8 us (15%)
  local copies, waits for them, and re-layouts  45 us (15%)
  matrix products  41 us (14%)
  starting transfers between devices  17.4 us (6%)
  between operations  14 us (5%)
    all_gather x1, waiting for transfers between devices, local(): lax.all_gather(spectral_in, 'lev', axis=3, tiled=True)  53.3 us
    all_to_all x1, blocking collectives, local(): lax.all_to_all(outgoing_waves, ('lat', 'lon'), split_axis=0, concat_axis=...  45.8 us
    reduce_sum x2, other arithmetic, absorbed_mean(): running = running + jnp.sum(terms, axis=0)  26.4 us
    dot_general x2, matrix products, transform(): partial = jnp.einsum('fdqn,wn->fdqw', sectors, dft_table, precision=highest)  17.8 us
    all_gather x1, waiting for transfers between devices, carried_in(): pieces = lax.all_gather(planes, axis)  15.3 us
    dot_general x1, matrix products, local(): jnp.einsum('mcfls,mns->mcfln', lax.all_gather(spectral_in, 'lev', axis=3,...  14.3 us
    all_to_all x2, starting transfers between devices, to_sectors(): return lax.all_to_all(lines, 'lon', split_axis=1, concat_axis=1, tiled=True)  10.5 us
    all_to_all x2, waiting for transfers between devices, to_sectors(): return lax.all_to_all(lines, 'lon', split_axis=1, concat_axis=1, tiled=True)  9.28 us
  transfers between devices with their start and end apart: 6, of which 5 were waited for; matrix products, arithmetic and copies ran while one was open for 26% of the time, Pallas kernels for 0%

commit v1 on v0

--- a/solution.py
+++ b/solution.py
@@ -98,9 +98,10 @@
     onehot = (
         source_ids[:, :, None] == jnp.arange(tile_count + 2, dtype=jnp.int32)[None, None, :]
     ).astype(jnp.float32)
-    blocks = (sl_weights[:, :, :, None, :] * onehot[:, :, None, :, None]).reshape(
-        row_blocks, lon_local, (tile_count + 2) * tile_width
-    )
+    lane_mask = jnp.repeat(onehot, tile_width, axis=-1) > 0.5
+    blocks = jnp.where(
+        lane_mask[:, :, None, :], jnp.tile(sl_weights, (1, 1, 1, tile_count + 2)), 0.0
+    ).reshape(row_blocks, lon_local, (tile_count + 2) * tile_width)
     padded_rows = padded.reshape(field_count, lev_local, row_blocks, block_rows, -1)
     departure_estimate = jnp.einsum(
         "flbrk,bnk->bflrn", padded_rows, blocks, precision=highest
@@ -176,13 +177,14 @@
         lat_count, lev_local, halves, 2, waves_local, field_count, chunk_rows
     )
     spectral_in = arrived.transpose(4, 3, 5, 1, 0, 2, 6).reshape(
-        waves_local, 2, field_count, lev_local, lat_count * lat_local
-    )
-    spectra = jnp.einsum(
-        "mcfls,mns->mcfln",
-        lax.all_gather(spectral_in, "lev", axis=3, tiled=True),
-        legendre,
-        precision=highest,
+        waves_local, 2 * field_count * lev_local, lat_count * lat_local
+    )
+    gathered = lax.all_gather(spectral_in, "lev", axis=0).transpose(1, 0, 2, 3)
+    spectra = jnp.einsum("skqp,snp->skqn", gathered, legendre, precision=highest)
+    spectra = (
+        spectra.reshape(waves_local, lev_count, 2, field_count, lev_local, -1)
+        .transpose(0, 2, 3, 1, 4, 5)
+        .reshape(waves_local, 2, field_count, lev_count * lev_local, -1)
     )
     degree_local = legendre.shape[1]
     degrees = lax.axis_index("lev") * degree_local + jnp.arange(degree_local, dtype=jnp.int32)

time: 300 us -> 300 us (level)
  local copies, waits for them, and re-layouts: 45 us -> 55.8 us
  waiting for transfers between devices: 83.7 us -> 78.7 us
  other arithmetic: 49.5 us -> 45.2 us
    another operation x0 -> x4, local copies, waits for them, and re-layouts: none -> 25.1 us  [the longest x3 20.4 us: local(): jnp.tile(sl_weights, (1, 1, 1, tile_count + 2))]
    mul x1 -> x0, local copies, waits for them, and re-layouts: 9.04 us -> none  [local(): sl_weights[:, :, :, None, :] * onehot[:, :, None, :, None]]
    reshape x2, local copies, waits for them, and re-layouts: 8.58 us -> 0.63 us  [the longest x1 0.34 us: local(): spectra = spectra.reshape(waves_local, lev_count, 2, field_count, lev_loc...]
    mul x1 -> x0, other arithmetic: 5.68 us -> none  [local(): sl_weights[:, :, :, None, :] * onehot[:, :, None, :, None]]
    dot_general x1, matrix products: 14.3 us -> 11.2 us  [local(): jnp.einsum('skqp,snp->skqn', gathered, legendre, precision=highest)]
  transfers between devices with their start and end apart: 6 -> 6, of which waited for: 5 -> 4; matrix products, arithmetic and copies ran while one was open for 26% -> 28% of each run, Pallas kernels for 0% -> 0%
where the time goes in v1:
time: 300 us; the launch traced here: 296 us
  waiting for transfers between devices  78.7 us (26%)
  local copies, waits for them, and re-layouts  55.8 us (19%)
  blocking collectives  45.8 us (15%)
  other arithmetic  45.2 us (15%)
  matrix products  38.2 us (13%)
  starting transfers between devices  17.9 us (6%)
  between operations  14 us (5%)
    all_gather x1, waiting for transfers between devices, local(): gathered = lax.all_gather(spectral_in, 'lev', axis=0).transpose(1, 0, 2, 3)  53.3 us
    all_to_all x1, blocking collectives, local(): lax.all_to_all(outgoing_waves, ('lat', 'lon'), split_axis=0, concat_axis=...  45.8 us
    reduce_sum x2, other arithmetic, absorbed_mean(): running = running + jnp.sum(terms, axis=0)  26.4 us
    another operation x3, local copies, waits for them, and re-layouts, local(): jnp.tile(sl_weights, (1, 1, 1, tile_count + 2))  20.4 us
    dot_general x2, matrix products, transform(): partial = jnp.einsum('fdqn,wn->fdqw', sectors, dft_table, precision=highest)  17.8 us
    all_gather x1, waiting for transfers between devices, carried_in(): pieces = lax.all_gather(planes, axis)  15.6 us
    dot_general x1, matrix products, local(): jnp.einsum('skqp,snp->skqn', gathered, legendre, precision=highest)  11.2 us
    all_to_all x2, starting transfers between devices, to_sectors(): return lax.all_to_all(lines, 'lon', split_axis=1, concat_axis=1, tiled=True)  11 us
  transfers between devices with their start and end apart: 6, of which 4 were waited for; matrix products, arithmetic and copies ran while one was open for 28% of the time, Pallas kernels for 0%

profile of v1, /device:TPU:1, one launch (start us, length us, event | category | flops | bytes accessed | tf_op | source)
XLA Modules:
  0.0 295.6 jit_solution(6916871664525365557)
XLA Ops:
  6.5 3.0 %fusion.52 = (f32[3,4,160,128]{3,2,1,0:T(8,128)}, f32[3,4,160,128]{3,2,1,0:T(8,128)}) fusion(f32[3,4,160,384]{3,2,1,0:T(8,128)} %param.9), kind=kLoop, calls=%fused_computation.106 | loop fusion | bytes 3932160 | tf_op jit(solution)/shard_map/slice | solution.py:20
  9.5 6.4 %collective-permute-start.1 = (f32[3,4,160,128]{3,2,1,0:T(8,128)}, f32[3,4,160,128]{3,2,1,0:T(8,128)}, u32[]{:S(2)}, u32[]{:S(2)}) collective-permute-start(f32[3,4,160,128]{3,2,1,0:T(8,128)} %get-tuple-element.37), channel_id=1, source_target_pairs={{4,0},{8,4},{12,8},{16,12},{20,16},{24,20},{28,24},{0,28},{5,1},{9... | collective-permute-start | bytes 2949128 | tf_op jit(solution)/shard_map/ppermute | solution.py:22
  15.9 0.8 broadcast_add_fusion
  17.0 1.9 copy.59
  18.9 4.2 %tile.4 = f32[5,3,1,128,5,128]{3,1,5,4,0,2:T(4,128)} broadcast(f32[5,3,128,128]{2,1,3,0:T(4,128)S(1)} %copy.59), dimensions={0,1,3,5} | broadcast | bytes 5898240 | tf_op jit(solution)/shard_map/tile | solution.py:103
  23.1 9.0 %tile.10 = f32[5,384,640]{1,2,0:T(8,128)} reshape(f32[5,3,1,128,5,128]{3,1,5,4,0,2:T(4,128)} %tile.4) | data formatting | bytes 9830400 | tf_op jit(solution)/shard_map/tile | solution.py:103
  32.1 7.1 %copy.60 = f32[5,384,640]{2,1,0:T(8,128)} copy(f32[5,384,640]{1,2,0:T(8,128)} %tile.10) | data formatting | bytes 9830400 | tf_op jit(solution)/shard_map/tile | solution.py:103
  39.3 0.5 collective-permute-done
  39.7 2.1 pad_maximum_fusion
  41.8 0.3 broadcast_in_dim.38
  42.2 9.2 %fusion.12 = f32[3,4,5,32,384]{4,3,1,0,2:T(8,128)S(1)} fusion(pred[5,384,640]{2,1,0:T(32,128)(4,1)S(1)} %bitcast.75, f32[5,384,640]{2,1,0:T(8,128)S(1)} %copy-done, f32[3,4,5,32,640]{4,3,2,1,0:T(8,128)S(1)} %bitcast.71), kind=kOutput, calls=%fused_computation.22 | convolution fusion | flops 5663539200 | bytes 14008320 | tf_op jit(solution)/shard_map/flbrk,bnk->bflrn/dot_general | solution.py:106
  51.5 1.8 fusion.45
  53.3 0.8 pad_maximum_fusion.6
  54.6 0.5 iota_compare_fusion.1
  55.8 1.5 copy.68
  57.2 4.3 %all-to-all-start.1 = ((f32[2,8,80,384]{3,2,0,1:T(8,128)}), f32[2,8,80,384]{3,2,0,1:T(8,128)S(1)}, u32[]{:S(2)}, u32[]{:S(2)}) async-start(f32[2,8,80,384]{3,2,0,1:T(8,128)} %copy.68), calls=%async_computation.1 | async-start | bytes 3932160 | tf_op jit(solution)/shard_map/all_to_all | solution.py:142
  61.5 2.2 copy.62
  63.8 1.0 copy.64
  64.8 2.3 copy.63
  67.1 2.3 fusion.53
  69.4 15.6 %all-gather.6.cloned.1.call-done = f32[8,160,384]{2,1,0:T(8,128)} async-done(((f32[2,160,384]{2,1,0:T(8,128)}), f32[8,160,384]{2,1,0:T(8,128)}) %all-gather.6.cloned.1.call-update) | async-done | bytes 1966096 | tf_op jit(solution)/shard_map/all_gather | solution.py:29
  85.0 1.9 select_reduce_fusion
  86.9 1.5 fusion.49
  88.6 13.2 %multiply_reduce_fusion.3 = (f32[4,160,384]{2,1,0:T(8,128)S(1)}, f32[4,160,384]{2,1,0:T(8,128)S(1)}) fusion(f32[8]{0:T(128)S(1)} %get-tuple-element.73, f32[8]{0:T(128)S(1)} %get-tuple-element.74, f32[8]{0:T(128)S(1)} %get-tuple-element.75, f32[4,160,384]{2,1,0:T(8,128)S(1)} %bitcast.82, f32[4,160,384]{2,1,0:T(8,128)S(1)} %bitcast.84, ...), kind=kLoop, calls=%fused_computation.5 | loop fusion | flops 74219520 | bytes 5898688 | tf_op jit(solution)/shard_map/reduce_sum | solution.py:82
  101.8 13.2 %multiply_reduce_fusion.2 = (f32[4,160,384]{2,1,0:T(8,128)S(1)}, f32[4,160,384]{2,1,0:T(8,128)S(1)}) fusion(f32[8]{0:T(128)S(1)} %get-tuple-element.70, f32[8]{0:T(128)S(1)} %get-tuple-element.71, f32[8]{0:T(128)S(1)} %get-tuple-element.72, f32[8]{0:T(128)S(1)} %get-tuple-element.82, f32[8]{0:T(128)S(1)} %get-tuple-element.84, f32[8]{0:T(128)S(1)} %get-tuple-element.66, ...), kind=kLoop, calls=%fused_computation.4 | loop fusion | flops 74219520 | bytes 5898688 | tf_op jit(solution)/shard_map/reduce_sum | solution.py:82
  115.2 1.0 add_bitcast_fusion
  116.2 6.7 %all-to-all-start = ((f32[1,8,80,384]{3,2,0,1:T(8,128)}), f32[1,8,80,384]{3,2,0,1:T(8,128)S(1)}, u32[]{:S(2)}, u32[]{:S(2)}) async-start(f32[1,8,80,384]{3,2,0,1:T(8,128)} %add_bitcast_fusion), calls=%async_computation | async-start | bytes 1966080 | tf_op jit(solution)/shard_map/all_to_all | solution.py:142
  123.0 0.4 all-gather.4.cloned.1.call-start
  123.5 4.1 %cosine_multiply_fusion = (f32[640,384]{1,0:T(8,128)S(1)}, f32[640,384]{1,0:T(8,128)S(1)}) fusion(s32[640]{0:T(1024)S(1)} %copy-done.9), kind=kLoop, calls=%fused_computation.37 | loop fusion | flops 2703360 | bytes 1968640 | tf_op jit(solution)/shard_map/mul | solution.py:152
  127.7 12.2 %fusion.8 = f32[2,8,80,1280]{3,2,1,0:T(8,128)S(1)} fusion(f32[2,8,80,384]{3,2,0,1:T(8,128)} %copy-done.2, f32[640,384]{1,0:T(8,128)S(1)} %get-tuple-element.52, f32[640,384]{1,0:T(8,128)S(1)} %get-tuple-element.51), kind=kOutput, calls=%fused_computation.17 | convolution fusion | flops 7550238720 | bytes 10485760 | tf_op jit(solution)/shard_map/fdqn,wn->fdqw/dot_general | solution.py:159
  139.9 1.7 subtract_reduce_fusion
  141.6 9.3 %all-to-all-done = f32[1,8,80,384]{3,2,0,1:T(8,128)S(1)} async-done(((f32[1,8,80,384]{3,2,0,1:T(8,128)}), f32[1,8,80,384]{3,2,0,1:T(8,128)S(1)}, u32[]{:S(2)}, u32[]{:S(2)}) %all-to-all-start) | async-done | bytes 983072 | tf_op jit(solution)/shard_map/all_to_all | solution.py:142
  150.8 5.6 %convolution_bitcast_fusion = f32[1,8,80,1280]{3,2,1,0:T(8,128)S(1)} fusion(f32[640,384]{1,0:T(8,128)S(1)} %get-tuple-element.52, f32[640,384]{1,0:T(8,128)S(1)} %get-tuple-element.51, f32[1,8,80,384]{3,2,0,1:T(8,128)S(1)} %all-to-all-done), kind=kOutput, calls=%fused_computation.12 | convolution fusion | flops 3775365120 | bytes 6225920 | tf_op jit(solution)/shard_map/fdqn,wn->fdqw/dot_general | solution.py:159
  156.4 0.5 subtract_reduce_fusion.1
  157.1 2.5 copy.71
  159.6 2.9 copy.80
  162.5 2.0 reshape.379
  164.5 45.8 %all_to_all.15 = f32[64,20,240]{2,1,0:T(8,128)S(1)} all-to-all(f32[64,20,240]{2,1,0:T(8,128)} %reshape.379), channel_id=1, replica_groups=mesh['lat'=8,'lon'=8,'lev'=4] {'lat','lon'}, dimensions={0} | all-to-all | bytes 2457600 | tf_op jit(solution)/shard_map/all_to_all | solution.py:173
  210.2 1.5 copy.74
  211.7 2.9 reshape.366
  214.6 2.4 copy.75
  217.0 4.8 %all_gather_reshape.3 = f32[1,10,24,1280]{3,2,0,1:T(8,128)} reshape(f32[10,2,3,4,8,2,80]{6,5,4,3,2,1,0:T(2,128)} %copy.75) | data formatting | bytes 2457600 | tf_op jit(solution)/shard_map/all_gather;reshape | solution.py:182
  222.0 53.3 %all-gather.4.cloned.1.call-done = f32[4,10,24,1280]{3,2,0,1:T(8,128)} async-done(((f32[1,10,24,1280]{3,2,0,1:T(8,128)}), f32[4,10,24,1280]{3,2,0,1:T(8,128)}) %all-gather.4.cloned.1.call-update) | async-done | bytes 4915216 | tf_op jit(solution)/shard_map/all_gather | solution.py:182
  275.3 11.2 %fusion = f32[10,4,24,160]{3,2,1,0:T(8,128)S(1)} fusion(f32[10,160,1280]{2,1,0:T(8,128)} %param.17, f32[4,10,24,1280]{3,2,0,1:T(8,128)} %all-gather.4.cloned.1.call-done), kind=kOutput, calls=%fused_computation | convolution fusion | flops 2359296000 | bytes 13721600 | tf_op jit(solution)/shard_map/skqp,snp->skqn/dot_general | solution.py:183
  286.5 0.3 reshape.367
  286.8 0.3 copy.76
  287.1 0.3 reshape.368
  287.4 1.1 broadcast_select_fusion
  (58 shorter events, 2.2 us)
Async XLA Ops:
  6.5 78.4 %all-gather.6.cloned.1.call-start = ((), (), s32[]{:S(2)}) async-start(), calls=%async_computation.4 | async-start | bytes 2457600 | tf_op jit(solution)/shard_map/all_gather | solution.py:29
  9.5 29.8 %collective-permute-start.1 = (f32[3,4,160,128]{3,2,1,0:T(8,128)}, f32[3,4,160,128]{3,2,1,0:T(8,128)}, u32[]{:S(2)}, u32[]{:S(2)}) collective-permute-start(f32[3,4,160,128]{3,2,1,0:T(8,128)} %get-tuple-element.37), channel_id=1, source_target_pairs={{4,0},{8,4},{12,8},{16,12},{20,16},{24,20},{28,24},{0,28},{5,1},{9... | collective-permute-start | bytes 2949128 | tf_op jit(solution)/shard_map/ppermute | solution.py:22
  15.9 23.8 %collective-permute-start = (f32[3,4,160,128]{3,2,1,0:T(8,128)}, f32[3,4,160,128]{3,2,1,0:T(8,128)}, u32[]{:S(2)}, u32[]{:S(2)}) collective-permute-start(f32[3,4,160,128]{3,2,1,0:T(8,128)} %get-tuple-element.36), channel_id=1, source_target_pairs={{0,4},{4,8},{8,12},{12,16},{16,20},{20,24},{24,28},{28,0},{1,5},{5... | collective-permute-start | bytes 2949128 | tf_op jit(solution)/shard_map/ppermute | solution.py:19
  23.1 16.7 %copy-start.1 = (f32[3,4,160,384]{3,2,1,0:T(8,128)S(1)}, f32[3,4,160,384]{3,2,1,0:T(8,128)}, u32[]{:S(2)}) copy-start(f32[3,4,160,384]{3,2,1,0:T(8,128)} %param.9) | copy-start | bytes 8847364
  39.3 3.0 %copy-start = (f32[5,384,640]{2,1,0:T(8,128)S(1)}, f32[5,384,640]{2,1,0:T(8,128)}, u32[]{:S(2)}) copy-start(f32[5,384,640]{2,1,0:T(8,128)} %copy.60) | copy-start | bytes 14745604
  42.2 11.9 %copy-start.12 = (s32[160,3]{0,1:T(4,128)S(1)}, s32[160,3]{0,1:T(4,128)}, u32[]{:S(2)}) copy-start(s32[160,3]{0,1:T(4,128)} %param.12) | copy-start | bytes 5764
  51.5 3.6 %copy-start.11 = (f32[32]{0:T(128)S(1)}, f32[32]{0:T(128)}, u32[]{:S(2)}) copy-start(f32[32]{0:T(128)} %param.14) | copy-start | bytes 388
  51.5 3.7 %copy-start.8 = (f32[32]{0:T(128)S(1)}, f32[32]{0:T(128)}, u32[]{:S(2)}) copy-start(f32[32]{0:T(128)} %param.15) | copy-start | bytes 388
  51.5 3.8 %copy-start.10 = (f32[32]{0:T(128)S(1)}, f32[32]{0:T(128)}, u32[]{:S(2)}) copy-start(f32[32]{0:T(128)} %param.13) | copy-start | bytes 388
  55.6 8.2 %copy-start.3 = (f32[1,4,5,32,384]{4,3,1,0,2:T(8,128)S(1)}, f32[1,4,5,32,384]{4,3,1,0,2:T(8,128)}, u32[]{:S(2)}) copy-start(f32[1,4,5,32,384]{4,3,1,0,2:T(8,128)} %get-tuple-element.33) | copy-start | bytes 2949124
  57.2 59.0 %all-to-all-start.1 = ((f32[2,8,80,384]{3,2,0,1:T(8,128)}), f32[2,8,80,384]{3,2,0,1:T(8,128)S(1)}, u32[]{:S(2)}, u32[]{:S(2)}) async-start(f32[2,8,80,384]{3,2,0,1:T(8,128)} %copy.68), calls=%async_computation.1 | async-start | bytes 3932160 | tf_op jit(solution)/shard_map/all_to_all | solution.py:142
  69.4 19.2 %copy-start.6 = (f32[1,4,5,32,384]{4,3,2,1,0:T(8,128)S(1)}, f32[1,4,5,32,384]{4,3,2,1,0:T(8,128)}, u32[]{:S(2)}) copy-start(f32[1,4,5,32,384]{4,3,2,1,0:T(8,128)} %copy.64) | copy-start | bytes 2949124
  85.0 3.6 %copy-start.7 = (f32[1,4,5,32,384]{4,3,2,1,0:T(8,128)S(1)}, f32[1,4,5,32,384]{4,3,2,1,0:T(8,128)}, u32[]{:S(2)}) copy-start(f32[1,4,5,32,384]{4,3,2,1,0:T(8,128)} %copy.63) | copy-start | bytes 2949124
  101.7 13.4 %copy-start.4 = (f32[1,4,5,32,384]{4,3,2,1,0:T(8,128)S(1)}, f32[1,4,5,32,384]{4,3,2,1,0:T(8,128)}, u32[]{:S(2)}) copy-start(f32[1,4,5,32,384]{4,3,2,1,0:T(8,128)} %copy.62) | copy-start | bytes 2949124
  114.9 8.5 %copy-start.9 = (s32[640]{0:T(1024)S(1)}, s32[640]{0:T(1024)}, u32[]{:S(2)}) copy-start(s32[640]{0:T(1024)} %param.16) | copy-start | bytes 7684
  116.2 7.2 %copy-start.2 = (f32[2,8,80,384]{3,2,0,1:T(8,128)}, f32[2,8,80,384]{3,2,0,1:T(8,128)S(1)}, u32[]{:S(2)}) copy-start(f32[2,8,80,384]{3,2,0,1:T(8,128)S(1)} %all-to-all-done.1) | copy-start | bytes 5898244
  116.2 34.6 %all-to-all-start = ((f32[1,8,80,384]{3,2,0,1:T(8,128)}), f32[1,8,80,384]{3,2,0,1:T(8,128)S(1)}, u32[]{:S(2)}, u32[]{:S(2)}) async-start(f32[1,8,80,384]{3,2,0,1:T(8,128)} %add_bitcast_fusion), calls=%async_computation | async-start | bytes 1966080 | tf_op jit(solution)/shard_map/all_to_all | solution.py:142
  123.0 152.3 %all-gather.4.cloned.1.call-start = ((), (), s32[]{:S(2)}) async-start(), calls=%async_computation.3 | async-start | bytes 6144000 | tf_op jit(solution)/shard_map/all_gather | solution.py:182
  150.8 6.1 %copy-start.5 = (f32[2,80,640]{2,1,0:T(8,128)S(1)}, f32[2,80,640]{2,1,0:T(8,128)}, u32[]{:S(2)}) copy-start(f32[2,80,640]{2,1,0:T(8,128)} %get-tuple-element.5) | copy-start | bytes 1228804
Sparse Core Ops, SparseCore 0:
  54.3 30.6 all-gather.5
  222.0 53.3 all-gather.3

commit v2 on v1

--- a/solution.py
+++ b/solution.py
@@ -179,7 +179,16 @@
     spectral_in = arrived.transpose(4, 3, 5, 1, 0, 2, 6).reshape(
         waves_local, 2 * field_count * lev_local, lat_count * lat_local
     )
-    gathered = lax.all_gather(spectral_in, "lev", axis=0).transpose(1, 0, 2, 3)
+    lev_here = lax.axis_index("lev")
+    pieces = [spectral_in]
+    for shift in range(1, lev_count):
+        pieces.append(
+            lax.ppermute(
+                spectral_in, "lev", [(k, (k + shift) % lev_count) for k in range(lev_count)]
+            )
+        )
+    by_offset = jnp.stack([pieces[(-t) % lev_count] for t in range(lev_count)] * 2, axis=1)
+    gathered = lax.dynamic_slice_in_dim(by_offset, lev_count - lev_here, lev_count, axis=1)
     spectra = jnp.einsum("skqp,snp->skqn", gathered, legendre, precision=highest)
     spectra = (
         spectra.reshape(waves_local, lev_count, 2, field_count, lev_local, -1)

time: 300 us -> 306 us (1.020)
  local copies, waits for them, and re-layouts: 55.8 us -> 63.7 us
  waiting for transfers between devices: 78.7 us -> 71.2 us
  starting transfers between devices: 17.9 us -> 25.1 us
    all_gather x1 -> x0, waiting for transfers between devices: 53.3 us -> none  [local(): gathered = lax.all_gather(spectral_in, 'lev', axis=0).transpose(1, 0, 2, 3)]
    ppermute x0 -> x3, waiting for transfers between devices: none -> 44.9 us  [local(): lax.ppermute(spectral_in, 'lev', [(k, (k + shift) % lev_count) for k in r...]
    unnamed x28 -> x43, local copies, waits for them, and re-layouts: 2.09 us -> 9.98 us
    ppermute x0 -> x3, starting transfers between devices: none -> 6.07 us  [local(): lax.ppermute(spectral_in, 'lev', [(k, (k + shift) % lev_count) for k in r...]
    reshape x0 -> x1, local copies, waits for them, and re-layouts: none -> 4.3 us  [local(): arrived.transpose(4, 3, 5, 1, 0, 2, 6)]
  transfers between devices with their start and end apart: 6 -> 8, of which waited for: 4 -> 5; matrix products, arithmetic and copies ran while one was open for 28% -> 29% of each run, Pallas kernels for 0% -> 0%
where the time goes in v2:
time: 306 us; the launch traced here: 300 us
  waiting for transfers between devices  71.2 us (23%)
  local copies, waits for them, and re-layouts  63.7 us (21%)
  blocking collectives  45.8 us (15%)
  other arithmetic  44.8 us (15%)
  matrix products  35.6 us (12%)
  starting transfers between devices  25.1 us (8%)
  between operations  14.2 us (5%)
    all_to_all x1, blocking collectives, local(): lax.all_to_all(outgoing_waves, ('lat', 'lon'), split_axis=0, concat_axis=...  45.8 us
    ppermute x3, waiting for transfers between devices, local(): lax.ppermute(spectral_in, 'lev', [(k, (k + shift) % lev_count) for k in r...  44.9 us
    reduce_sum x2, other arithmetic, absorbed_mean(): running = running + jnp.sum(terms, axis=0)  26.4 us
    another operation x3, local copies, waits for them, and re-layouts, local(): jnp.tile(sl_weights, (1, 1, 1, tile_count + 2))  20.2 us
    dot_general x2, matrix products, transform(): partial = jnp.einsum('fdqn,wn->fdqw', sectors, dft_table, precision=highest)  17.8 us
    all_gather x1, waiting for transfers between devices, carried_in(): pieces = lax.all_gather(planes, axis)  16.9 us
    all_to_all x2, starting transfers between devices, to_sectors(): return lax.all_to_all(lines, 'lon', split_axis=1, concat_axis=1, tiled=True)  12.6 us
    unnamed x43, local copies, waits for them, and re-layouts  9.98 us
  transfers between devices with their start and end apart: 8, of which 5 were waited for; matrix products, arithmetic and copies ran while one was open for 29% of the time, Pallas kernels for 0%

profile of v2, /device:TPU:1, one launch (start us, length us, event | category | flops | bytes accessed | tf_op | source)
XLA Modules:
  0.0 300.3 jit_solution(17154152333992573063)
XLA Ops:
  6.5 3.0 fusion.53
  9.5 2.5 collective-permute-start
  12.0 3.9 %collective-permute-start.1 = (f32[3,4,160,128]{3,2,1,0:T(8,128)}, f32[3,4,160,128]{3,2,1,0:T(8,128)S(1)}, u32[]{:S(2)}, u32[]{:S(2)}) collective-permute-start(f32[3,4,160,128]{3,2,1,0:T(8,128)} %get-tuple-element.37), channel_id=1, source_target_pairs={{4,0},{8,4},{12,8},{16,12},{20,16},{24,20},{28,24},{0,28},{5,1},{9... | collective-permute-start | bytes 2949128 | tf_op jit(solution)/shard_map/ppermute | solution.py:22
  15.9 1.9 copy.78
  17.9 4.2 %tile.4 = f32[5,3,1,128,5,128]{3,1,5,4,0,2:T(4,128)} broadcast(f32[5,3,128,128]{2,1,3,0:T(4,128)S(1)} %copy.78), dimensions={0,1,3,5} | broadcast | bytes 5898240 | tf_op jit(solution)/shard_map/tile | solution.py:103
  22.0 8.9 %tile.10 = f32[5,384,640]{1,2,0:T(8,128)} reshape(f32[5,3,1,128,5,128]{3,1,5,4,0,2:T(4,128)} %tile.4) | data formatting | bytes 9830400 | tf_op jit(solution)/shard_map/tile | solution.py:103
  30.9 7.1 %copy.79 = f32[5,384,640]{2,1,0:T(8,128)} copy(f32[5,384,640]{1,2,0:T(8,128)} %tile.10) | data formatting | bytes 9830400 | tf_op jit(solution)/shard_map/tile | solution.py:103
  38.5 2.5 pad_maximum_fusion
  41.6 9.6 %fusion.12 = f32[3,4,5,32,384]{4,3,1,0,2:T(8,128)S(1)} fusion(pred[5,384,640]{2,1,0:T(32,128)(4,1)S(1)} %bitcast.91, f32[5,384,640]{2,1,0:T(8,128)S(1)} %bitcast.84, f32[3,4,5,32,640]{4,3,2,1,0:T(8,128)S(1)} %bitcast.85), kind=kOutput, calls=%fused_computation.22 | convolution fusion | flops 5663539200 | bytes 14008320 | tf_op jit(solution)/shard_map/flbrk,bnk->bflrn/dot_general | solution.py:106
  51.2 1.6 copy-done
  52.8 1.6 fusion.46
  56.6 2.2 copy.82
  58.8 1.1 copy.83
  59.8 1.0 copy.81
  61.0 1.4 copy.87
  62.5 5.5 %all-to-all-start.1 = ((f32[2,8,80,384]{3,2,0,1:T(8,128)}), f32[2,8,80,384]{3,2,0,1:T(8,128)S(1)}, u32[]{:S(2)}, u32[]{:S(2)}) async-start(f32[2,8,80,384]{3,2,0,1:T(8,128)} %copy.87), calls=%async_computation.1 | async-start | bytes 3932160 | tf_op jit(solution)/shard_map/all_to_all | solution.py:142
  68.0 2.3 fusion.54
  70.3 16.9 %all-gather.3.cloned.1.call-done = f32[8,160,384]{2,1,0:T(8,128)} async-done(((f32[2,160,384]{2,1,0:T(8,128)}), f32[8,160,384]{2,1,0:T(8,128)}) %all-gather.3.cloned.1.call-update) | async-done | bytes 1966096 | tf_op jit(solution)/shard_map/all_gather | solution.py:29
  87.2 1.9 select_reduce_fusion
  89.1 1.5 fusion.50
  90.8 13.2 %multiply_reduce_fusion.2 = (f32[4,160,384]{2,1,0:T(8,128)S(1)}, f32[4,160,384]{2,1,0:T(8,128)S(1)}) fusion(f32[8]{0:T(128)S(1)} %get-tuple-element.70, f32[8]{0:T(128)S(1)} %get-tuple-element.71, f32[8]{0:T(128)S(1)} %get-tuple-element.72, f32[8]{0:T(128)S(1)} %get-tuple-element.82, f32[8]{0:T(128)S(1)} %get-tuple-element.84, f32[8]{0:T(128)S(1)} %get-tuple-element.66, ...), kind=kLoop, calls=%fused_computation.4 | loop fusion | flops 74219520 | bytes 5898688 | tf_op jit(solution)/shard_map/reduce_sum | solution.py:82
  104.0 13.2 %multiply_reduce_fusion.3 = (f32[4,160,384]{2,1,0:T(8,128)S(1)}, f32[4,160,384]{2,1,0:T(8,128)S(1)}) fusion(f32[8]{0:T(128)S(1)} %get-tuple-element.73, f32[8]{0:T(128)S(1)} %get-tuple-element.74, f32[8]{0:T(128)S(1)} %get-tuple-element.75, f32[4,160,384]{2,1,0:T(8,128)S(1)} %bitcast.101, f32[4,160,384]{2,1,0:T(8,128)S(1)} %bitcast.99, ...), kind=kLoop, calls=%fused_computation.5 | loop fusion | flops 74219520 | bytes 5898688 | tf_op jit(solution)/shard_map/reduce_sum | solution.py:82
  117.4 1.0 add_bitcast_fusion
  118.5 7.1 %all-to-all-start = ((f32[1,8,80,384]{3,2,0,1:T(8,128)}), f32[1,8,80,384]{3,2,0,1:T(8,128)S(1)}, u32[]{:S(2)}, u32[]{:S(2)}) async-start(f32[1,8,80,384]{3,2,0,1:T(8,128)} %add_bitcast_fusion), calls=%async_computation | async-start | bytes 1966080 | tf_op jit(solution)/shard_map/all_to_all | solution.py:142
  125.7 4.1 %cosine_multiply_fusion = (f32[640,384]{1,0:T(8,128)S(1)}, f32[640,384]{1,0:T(8,128)S(1)}) fusion(s32[640]{0:T(1024)S(1)} %copy-done.8), kind=kLoop, calls=%fused_computation.43 | loop fusion | flops 2703360 | bytes 1968640 | tf_op jit(solution)/shard_map/mul | solution.py:152
  129.8 12.2 %fusion.8 = f32[2,8,80,1280]{3,2,1,0:T(8,128)S(1)} fusion(f32[2,8,80,384]{3,2,0,1:T(8,128)} %copy-done.1, f32[640,384]{1,0:T(8,128)S(1)} %get-tuple-element.52, f32[640,384]{1,0:T(8,128)S(1)} %get-tuple-element.51), kind=kOutput, calls=%fused_computation.17 | convolution fusion | flops 7550238720 | bytes 10485760 | tf_op jit(solution)/shard_map/fdqn,wn->fdqw/dot_general | solution.py:159
  142.1 1.7 subtract_reduce_fusion
  143.7 9.3 %all-to-all-done = f32[1,8,80,384]{3,2,0,1:T(8,128)S(1)} async-done(((f32[1,8,80,384]{3,2,0,1:T(8,128)}), f32[1,8,80,384]{3,2,0,1:T(8,128)S(1)}, u32[]{:S(2)}, u32[]{:S(2)}) %all-to-all-start) | async-done | bytes 983072 | tf_op jit(solution)/shard_map/all_to_all | solution.py:142
  153.1 5.6 %convolution_bitcast_fusion = f32[1,8,80,1280]{3,2,1,0:T(8,128)S(1)} fusion(f32[640,384]{1,0:T(8,128)S(1)} %get-tuple-element.52, f32[640,384]{1,0:T(8,128)S(1)} %get-tuple-element.51, f32[1,8,80,384]{3,2,0,1:T(8,128)S(1)} %all-to-all-done), kind=kOutput, calls=%fused_computation.12 | convolution fusion | flops 3775365120 | bytes 6225920 | tf_op jit(solution)/shard_map/fdqn,wn->fdqw/dot_general | solution.py:159
  159.3 2.2 copy.90
  161.6 2.9 copy.104
  164.5 2.3 reshape.383
  166.7 45.8 %all_to_all.15 = f32[64,20,240]{2,1,0:T(8,128)S(1)} all-to-all(f32[64,20,240]{2,1,0:T(8,128)} %reshape.383), channel_id=1, replica_groups=mesh['lat'=8,'lon'=8,'lev'=4] {'lat','lon'}, dimensions={0} | all-to-all | bytes 2457600 | tf_op jit(solution)/shard_map/all_to_all | solution.py:173
  212.9 2.2 reshape.369
  215.1 2.8 copy.94
  217.9 4.3 %reshape.370 = f32[10,24,1280]{2,1,0:T(8,128)} reshape(f32[10,2,3,4,8,2,80]{6,5,4,3,2,1,0:T(2,128)S(1)} %copy.94) | data formatting | bytes 2457600 | tf_op jit(solution)/shard_map/reshape | solution.py:179
  222.2 4.1 %collective-permute-start.2 = (f32[10,24,1280]{2,1,0:T(8,128)}, f32[10,24,1280]{2,1,0:T(8,128)}, u32[]{:S(2)}, u32[]{:S(2)}) collective-permute-start(f32[10,24,1280]{2,1,0:T(8,128)} %reshape.370), channel_id=1, source_target_pairs={{0,3},{1,0},{2,1},{3,2},{4,7},{5,4},{6,5},{7,6},{8,11},{9,8},{10,9... | collective-permute-start | bytes 3686408 | tf_op jit(solution)/shard_map/ppermute | solution.py:186
  226.5 3.2 %stack_reshape.4 = f32[10,1,24,1280]{3,2,1,0:T(8,128)S(1)} reshape(f32[10,2,3,4,8,2,80]{6,5,4,3,2,1,0:T(2,128)S(1)} %copy.94) | data formatting | bytes 2457600 | tf_op jit(solution)/shard_map/stack;reshape | solution.py:190
  229.7 1.9 collective-permute-start.4
  231.8 20.9 %collective-permute-done.2 = f32[10,24,1280]{2,1,0:T(8,128)} collective-permute-done((f32[10,24,1280]{2,1,0:T(8,128)}, f32[10,24,1280]{2,1,0:T(8,128)}, u32[]{:S(2)}, u32[]{:S(2)}) %collective-permute-start.2) | collective-permute-done | bytes 1228832 | tf_op jit(solution)/shard_map/ppermute | solution.py:186
  252.7 1.5 bitcast_dynamic-update-slice_fusion.2
  254.2 1.5 collective-permute-done.3
  255.7 1.4 bitcast_dynamic-update-slice_fusion
  257.1 22.5 %collective-permute-done.4 = f32[10,24,1280]{2,1,0:T(8,128)S(1)} collective-permute-done((f32[10,24,1280]{2,1,0:T(8,128)}, f32[10,24,1280]{2,1,0:T(8,128)S(1)}, u32[]{:S(2)}, u32[]{:S(2)}) %collective-permute-start.4) | collective-permute-done | bytes 1228832 | tf_op jit(solution)/shard_map/ppermute | solution.py:186
  279.9 1.5 bitcast_dynamic-update-slice_fusion.3
  281.4 1.4 bitcast_dynamic-update-slice_fusion.1
  283.0 8.3 %fusion = f32[10,4,24,160]{3,2,1,0:T(8,128)S(1)} fusion(f32[10,160,1280]{2,1,0:T(8,128)S(1)} %bitcast.88, f32[10,8,24,1280]{3,2,1,0:T(8,128)S(1)} %bitcast_dynamic-update-slice_fusion.5, s32[]{:T(128)S(6)} %select_n.41), kind=kOutput, calls=%fused_computation | convolution fusion | flops 2359296000 | bytes 13721604 | tf_op jit(solution)/shard_map/skqp,snp->skqn/dot_general | solution.py:192
  292.1 1.1 broadcast_select_fusion
  (81 shorter events, 6.3 us)
Async XLA Ops:
  6.5 80.7 %all-gather.3.cloned.1.call-start = ((), (), s32[]{:S(2)}) async-start(), calls=%async_computation.3 | async-start | bytes 2457600 | tf_op jit(solution)/shard_map/all_gather | solution.py:29
  9.5 29.0 %collective-permute-start = (f32[3,4,160,128]{3,2,1,0:T(8,128)}, f32[3,4,160,128]{3,2,1,0:T(8,128)S(1)}, u32[]{:S(2)}, u32[]{:S(2)}) collective-permute-start(f32[3,4,160,128]{3,2,1,0:T(8,128)} %get-tuple-element.36), channel_id=1, source_target_pairs={{0,4},{4,8},{8,12},{12,16},{16,20},{20,24},{24,28},{28,0},{1,5},{5... | collective-permute-start | bytes 2949128 | tf_op jit(solution)/shard_map/ppermute | solution.py:19
  12.0 26.5 %collective-permute-start.1 = (f32[3,4,160,128]{3,2,1,0:T(8,128)}, f32[3,4,160,128]{3,2,1,0:T(8,128)S(1)}, u32[]{:S(2)}, u32[]{:S(2)}) collective-permute-start(f32[3,4,160,128]{3,2,1,0:T(8,128)} %get-tuple-element.37), channel_id=1, source_target_pairs={{4,0},{8,4},{12,8},{16,12},{20,16},{24,20},{28,24},{0,28},{5,1},{9... | collective-permute-start | bytes 2949128 | tf_op jit(solution)/shard_map/ppermute | solution.py:22
  22.0 16.1 %copy-start.12 = (s32[5,3]{0,1:T(4,128)S(1)}, s32[5,3]{0,1:T(4,128)}, u32[]{:S(2)}) copy-start(s32[5,3]{0,1:T(4,128)} %param.11) | copy-start | bytes 184
  38.0 3.3 %slice-start = ((s8[4915200]{0:T(1024)(128)(4,1)}), s8[720896]{0:T(1024)(128)(4,1)S(1)}, s32[]{:S(2)}) async-start(s8[4915200]{0:T(1024)(128)(4,1)} %bitcast.83), calls=%async_computation.4 | async-start | bytes 1441792
  38.5 3.1 %slice-start.1 = ((s8[4915200]{0:T(1024)(128)(4,1)}), s8[4194304]{0:T(1024)(128)(4,1)S(1)}, s32[]{:S(2)}) async-start(s8[4915200]{0:T(1024)(128)(4,1)} %bitcast.83), calls=%async_computation.5 | async-start | bytes 8388608
  41.6 13.6 %copy-start.11 = (s32[160,3]{0,1:T(4,128)S(1)}, s32[160,3]{0,1:T(4,128)}, u32[]{:S(2)}) copy-start(s32[160,3]{0,1:T(4,128)} %param.12) | copy-start | bytes 5764
  51.2 1.6 copy-start
  52.8 3.5 %copy-start.10 = (f32[32]{0:T(128)S(1)}, f32[32]{0:T(128)}, u32[]{:S(2)}) copy-start(f32[32]{0:T(128)} %param.14) | copy-start | bytes 388
  52.8 3.5 %copy-start.7 = (f32[32]{0:T(128)S(1)}, f32[32]{0:T(128)}, u32[]{:S(2)}) copy-start(f32[32]{0:T(128)} %param.15) | copy-start | bytes 388
  52.8 3.6 %copy-start.9 = (f32[32]{0:T(128)S(1)}, f32[32]{0:T(128)}, u32[]{:S(2)}) copy-start(f32[32]{0:T(128)} %param.13) | copy-start | bytes 388
  54.4 6.5 %slice-start.2 = ((f32[3,4,5,32,384]{4,3,1,0,2:T(8,128)}), f32[2,4,5,32,384]{4,3,1,0,2:T(8,128)S(1)}, s32[]{:S(2)}) async-start(f32[3,4,5,32,384]{4,3,1,0,2:T(8,128)} %copy-done), calls=%async_computation.6 | async-start | bytes 3932160 | tf_op jit(solution)/shard_map/slice | solution.py:144
  55.4 4.5 %copy-start.3 = (f32[1,4,5,32,384]{4,3,1,0,2:T(8,128)S(1)}, f32[1,4,5,32,384]{4,3,1,0,2:T(8,128)}, u32[]{:S(2)}) copy-start(f32[1,4,5,32,384]{4,3,1,0,2:T(8,128)} %get-tuple-element.35) | copy-start | bytes 2949124
  62.5 56.0 %all-to-all-start.1 = ((f32[2,8,80,384]{3,2,0,1:T(8,128)}), f32[2,8,80,384]{3,2,0,1:T(8,128)S(1)}, u32[]{:S(2)}, u32[]{:S(2)}) async-start(f32[2,8,80,384]{3,2,0,1:T(8,128)} %copy.87), calls=%async_computation.1 | async-start | bytes 3932160 | tf_op jit(solution)/shard_map/all_to_all | solution.py:142
  70.3 20.4 %copy-start.5 = (f32[1,4,5,32,384]{4,3,2,1,0:T(8,128)S(1)}, f32[1,4,5,32,384]{4,3,2,1,0:T(8,128)}, u32[]{:S(2)}) copy-start(f32[1,4,5,32,384]{4,3,2,1,0:T(8,128)} %copy.82) | copy-start | bytes 2949124
  87.2 3.6 %copy-start.6 = (f32[1,4,5,32,384]{4,3,2,1,0:T(8,128)S(1)}, f32[1,4,5,32,384]{4,3,2,1,0:T(8,128)}, u32[]{:S(2)}) copy-start(f32[1,4,5,32,384]{4,3,2,1,0:T(8,128)} %copy.83) | copy-start | bytes 2949124
  104.0 13.4 %copy-start.2 = (f32[1,4,5,32,384]{4,3,2,1,0:T(8,128)S(1)}, f32[1,4,5,32,384]{4,3,2,1,0:T(8,128)}, u32[]{:S(2)}) copy-start(f32[1,4,5,32,384]{4,3,2,1,0:T(8,128)} %copy.81) | copy-start | bytes 2949124
  117.2 8.4 %copy-start.8 = (s32[640]{0:T(1024)S(1)}, s32[640]{0:T(1024)}, u32[]{:S(2)}) copy-start(s32[640]{0:T(1024)} %param.16) | copy-start | bytes 7684
  118.5 7.1 %copy-start.1 = (f32[2,8,80,384]{3,2,0,1:T(8,128)}, f32[2,8,80,384]{3,2,0,1:T(8,128)S(1)}, u32[]{:S(2)}) copy-start(f32[2,8,80,384]{3,2,0,1:T(8,128)S(1)} %all-to-all-done.1) | copy-start | bytes 5898244
  118.5 34.6 %all-to-all-start = ((f32[1,8,80,384]{3,2,0,1:T(8,128)}), f32[1,8,80,384]{3,2,0,1:T(8,128)S(1)}, u32[]{:S(2)}, u32[]{:S(2)}) async-start(f32[1,8,80,384]{3,2,0,1:T(8,128)} %add_bitcast_fusion), calls=%async_computation | async-start | bytes 1966080 | tf_op jit(solution)/shard_map/all_to_all | solution.py:142
  153.1 6.1 %copy-start.4 = (f32[2,80,640]{2,1,0:T(8,128)S(1)}, f32[2,80,640]{2,1,0:T(8,128)}, u32[]{:S(2)}) copy-start(f32[2,80,640]{2,1,0:T(8,128)} %get-tuple-element.5) | copy-start | bytes 1228804
  222.2 30.5 %collective-permute-start.2 = (f32[10,24,1280]{2,1,0:T(8,128)}, f32[10,24,1280]{2,1,0:T(8,128)}, u32[]{:S(2)}, u32[]{:S(2)}) collective-permute-start(f32[10,24,1280]{2,1,0:T(8,128)} %reshape.370), channel_id=1, source_target_pairs={{0,3},{1,0},{2,1},{3,2},{4,7},{5,4},{6,5},{7,6},{8,11},{9,8},{10,9... | collective-permute-start | bytes 3686408 | tf_op jit(solution)/shard_map/ppermute | solution.py:186
  226.3 29.4 %collective-permute-start.3 = (f32[10,24,1280]{2,1,0:T(8,128)}, f32[10,24,1280]{2,1,0:T(8,128)}, u32[]{:S(2)}, u32[]{:S(2)}) collective-permute-start(f32[10,24,1280]{2,1,0:T(8,128)} %reshape.370), channel_id=1, source_target_pairs={{0,2},{1,3},{2,0},{3,1},{4,6},{5,7},{6,4},{7,5},{8,10},{9,11},{10,... | collective-permute-start | bytes 3686408 | tf_op jit(solution)/shard_map/ppermute | solution.py:186
  229.7 49.9 %collective-permute-start.4 = (f32[10,24,1280]{2,1,0:T(8,128)}, f32[10,24,1280]{2,1,0:T(8,128)S(1)}, u32[]{:S(2)}, u32[]{:S(2)}) collective-permute-start(f32[10,24,1280]{2,1,0:T(8,128)} %reshape.370), channel_id=1, source_target_pairs={{0,1},{1,2},{2,3},{3,0},{4,5},{5,6},{6,7},{7,4},{8,9},{9,10},{10,1... | collective-permute-start | bytes 3686408 | tf_op jit(solution)/shard_map/ppermute | solution.py:186
  252.7 30.3 %slice-start.3 = ((s8[8192000]{0:T(1024)(128)(4,1)}), s8[4194304]{0:T(1024)(128)(4,1)S(1)}, s32[]{:S(2)}) async-start(s8[8192000]{0:T(1024)(128)(4,1)} %bitcast.87), calls=%async_computation.7 | async-start | bytes 8388608
  279.8 3.2 %slice-start.4 = ((s8[8192000]{0:T(1024)(128)(4,1)}), s8[3997696]{0:T(1024)(128)(4,1)S(1)}, s32[]{:S(2)}) async-start(s8[8192000]{0:T(1024)(128)(4,1)} %bitcast.87), calls=%async_computation.8 | async-start | bytes 7995392
Sparse Core Ops, SparseCore 0:
  55.3 31.8 all-gather.2

commit v3 on v1

--- a/solution.py
+++ b/solution.py
@@ -179,8 +179,18 @@
     spectral_in = arrived.transpose(4, 3, 5, 1, 0, 2, 6).reshape(
         waves_local, 2 * field_count * lev_local, lat_count * lat_local
     )
-    gathered = lax.all_gather(spectral_in, "lev", axis=0).transpose(1, 0, 2, 3)
-    spectra = jnp.einsum("skqp,snp->skqn", gathered, legendre, precision=highest)
+    lev_here = lax.axis_index("lev")
+
+    def swap(value, flip):
+        return lax.ppermute(value, "lev", [(k, k ^ flip) for k in range(lev_count)])
+
+    across = swap(spectral_in, 2)
+    by_flip = jnp.stack(
+        [spectral_in, swap(spectral_in, 1), across, swap(across, 1)], axis=1
+    )
+    flipped = jnp.einsum("skqp,snp->skqn", by_flip, legendre, precision=highest)
+    flipped = jnp.where((lev_here & 1) == 1, flipped[:, jnp.array([1, 0, 3, 2])], flipped)
+    spectra = jnp.where((lev_here & 2) == 2, flipped[:, jnp.array([2, 3, 0, 1])], flipped)
     spectra = (
         spectra.reshape(waves_local, lev_count, 2, field_count, lev_local, -1)
         .transpose(0, 2, 3, 1, 4, 5)

time: 300 us -> 280 us (0.933)
  waiting for transfers between devices: 78.7 us -> 45.7 us
  starting transfers between devices: 17.9 us -> 27.2 us
    all_gather x1 -> x0, waiting for transfers between devices: 53.3 us -> none  [local(): gathered = lax.all_gather(spectral_in, 'lev', axis=0).transpose(1, 0, 2, 3)]
    ppermute x0 -> x3, waiting for transfers between devices: none -> 20.4 us  [swap(): return lax.ppermute(value, 'lev', [(k, k ^ flip) for k in range(lev_count)])]
    ppermute x0 -> x3, starting transfers between devices: none -> 9.38 us  [swap(): return lax.ppermute(value, 'lev', [(k, k ^ flip) for k in range(lev_count)])]
    reshape x0 -> x1, local copies, waits for them, and re-layouts: none -> 4.27 us  [local(): arrived.transpose(4, 3, 5, 1, 0, 2, 6)]
  transfers between devices with their start and end apart: 6 -> 8, of which waited for: 4 -> 4; matrix products, arithmetic and copies ran while one was open for 28% -> 32% of each run, Pallas kernels for 0% -> 0%
where the time goes in v3:
time: 280 us; the launch traced here: 275 us
  local copies, waits for them, and re-layouts  58.4 us (21%)
  blocking collectives  45.8 us (16%)
  waiting for transfers between devices  45.7 us (16%)
  other arithmetic  45.5 us (16%)
  matrix products  38.3 us (14%)
  starting transfers between devices  27.2 us (10%)
  between operations  14.1 us (5%)
    all_to_all x1, blocking collectives, local(): lax.all_to_all(outgoing_waves, ('lat', 'lon'), split_axis=0, concat_axis=...  45.8 us
    reduce_sum x2, other arithmetic, absorbed_mean(): running = running + jnp.sum(terms, axis=0)  26.4 us
    ppermute x3, waiting for transfers between devices, swap(): return lax.ppermute(value, 'lev', [(k, k ^ flip) for k in range(lev_count)])  20.4 us
    another operation x3, local copies, waits for them, and re-layouts, local(): jnp.tile(sl_weights, (1, 1, 1, tile_count + 2))  20.4 us
    dot_general x2, matrix products, transform(): partial = jnp.einsum('fdqn,wn->fdqw', sectors, dft_table, precision=highest)  17.8 us
    all_gather x1, waiting for transfers between devices, carried_in(): pieces = lax.all_gather(planes, axis)  15.5 us
    all_to_all x2, starting transfers between devices, to_sectors(): return lax.all_to_all(lines, 'lon', split_axis=1, concat_axis=1, tiled=True)  11.4 us
    dot_general x1, matrix products, local(): flipped = jnp.einsum('skqp,snp->skqn', by_flip, legendre, precision=highest)  11.3 us
  transfers between devices with their start and end apart: 8, of which 4 were waited for; matrix products, arithmetic and copies ran while one was open for 32% of the time, Pallas kernels for 0%

profile of v3, /device:TPU:1, one launch (start us, length us, event | category | flops | bytes accessed | tf_op | source)
XLA Modules:
  0.0 275.0 jit_solution(710415403152466374)
XLA Ops:
  6.5 3.0 %fusion.59 = (f32[3,4,160,128]{3,2,1,0:T(8,128)}, f32[3,4,160,128]{3,2,1,0:T(8,128)}) fusion(f32[3,4,160,384]{3,2,1,0:T(8,128)} %param.11), kind=kLoop, calls=%fused_computation.119 | loop fusion | bytes 3932160 | tf_op jit(solution)/shard_map/slice | solution.py:20
  9.5 6.4 %collective-permute-start.1 = (f32[3,4,160,128]{3,2,1,0:T(8,128)}, f32[3,4,160,128]{3,2,1,0:T(8,128)}, u32[]{:S(2)}, u32[]{:S(2)}) collective-permute-start(f32[3,4,160,128]{3,2,1,0:T(8,128)} %get-tuple-element.37), channel_id=1, source_target_pairs={{4,0},{8,4},{12,8},{16,12},{20,16},{24,20},{28,24},{0,28},{5,1},{9... | collective-permute-start | bytes 2949128 | tf_op jit(solution)/shard_map/ppermute | solution.py:22
  15.9 0.8 broadcast_add_fusion
  17.0 1.9 copy.78
  18.9 4.2 %tile.4 = f32[5,3,1,128,5,128]{3,1,5,4,0,2:T(4,128)} broadcast(f32[5,3,128,128]{2,1,3,0:T(4,128)S(1)} %copy.78), dimensions={0,1,3,5} | broadcast | bytes 5898240 | tf_op jit(solution)/shard_map/tile | solution.py:103
  23.1 9.1 %tile.10 = f32[5,384,640]{1,2,0:T(8,128)} reshape(f32[5,3,1,128,5,128]{3,1,5,4,0,2:T(4,128)} %tile.4) | data formatting | bytes 9830400 | tf_op jit(solution)/shard_map/tile | solution.py:103
  32.2 7.1 %copy.79 = f32[5,384,640]{2,1,0:T(8,128)} copy(f32[5,384,640]{1,2,0:T(8,128)} %tile.10) | data formatting | bytes 9830400 | tf_op jit(solution)/shard_map/tile | solution.py:103
  39.3 0.4 collective-permute-done
  39.7 2.1 pad_maximum_fusion
  42.3 9.2 %fusion.18 = f32[3,4,5,32,384]{4,3,1,0,2:T(8,128)S(1)} fusion(pred[5,384,640]{2,1,0:T(32,128)(4,1)S(1)} %bitcast.83, f32[5,384,640]{2,1,0:T(8,128)S(1)} %copy-done, f32[3,4,5,32,640]{4,3,2,1,0:T(8,128)S(1)} %bitcast.79), kind=kOutput, calls=%fused_computation.30 | convolution fusion | flops 5663539200 | bytes 14008320 | tf_op jit(solution)/shard_map/flbrk,bnk->bflrn/dot_general | solution.py:106
  51.6 1.8 fusion.52
  53.4 0.8 pad_maximum_fusion.6
  54.6 0.6 iota_compare_fusion.1
  55.8 1.4 copy.87
  57.3 4.3 %all-to-all-start.1 = ((f32[2,8,80,384]{3,2,0,1:T(8,128)}), f32[2,8,80,384]{3,2,0,1:T(8,128)S(1)}, u32[]{:S(2)}, u32[]{:S(2)}) async-start(f32[2,8,80,384]{3,2,0,1:T(8,128)} %copy.87), calls=%async_computation.1 | async-start | bytes 3932160 | tf_op jit(solution)/shard_map/all_to_all | solution.py:142
  61.6 2.2 copy.81
  63.8 1.0 copy.83
  64.8 2.3 copy.82
  67.1 2.3 fusion.60
  69.4 15.5 %all-gather.3.cloned.1.call-done = f32[8,160,384]{2,1,0:T(8,128)} async-done(((f32[2,160,384]{2,1,0:T(8,128)}), f32[8,160,384]{2,1,0:T(8,128)}) %all-gather.3.cloned.1.call-update) | async-done | bytes 1966096 | tf_op jit(solution)/shard_map/all_gather | solution.py:29
  85.0 1.9 select_reduce_fusion
  86.9 1.5 fusion.56
  88.6 13.2 %multiply_reduce_fusion.3 = (f32[4,160,384]{2,1,0:T(8,128)S(1)}, f32[4,160,384]{2,1,0:T(8,128)S(1)}) fusion(f32[8]{0:T(128)S(1)} %get-tuple-element.73, f32[8]{0:T(128)S(1)} %get-tuple-element.74, f32[8]{0:T(128)S(1)} %get-tuple-element.75, f32[4,160,384]{2,1,0:T(8,128)S(1)} %bitcast.90, f32[4,160,384]{2,1,0:T(8,128)S(1)} %bitcast.92, ...), kind=kLoop, calls=%fused_computation.7 | loop fusion | flops 74219520 | bytes 5898688 | tf_op jit(solution)/shard_map/reduce_sum | solution.py:82
  101.8 13.2 %multiply_reduce_fusion.2 = (f32[4,160,384]{2,1,0:T(8,128)S(1)}, f32[4,160,384]{2,1,0:T(8,128)S(1)}) fusion(f32[8]{0:T(128)S(1)} %get-tuple-element.70, f32[8]{0:T(128)S(1)} %get-tuple-element.71, f32[8]{0:T(128)S(1)} %get-tuple-element.72, f32[8]{0:T(128)S(1)} %get-tuple-element.82, f32[8]{0:T(128)S(1)} %get-tuple-element.84, f32[8]{0:T(128)S(1)} %get-tuple-element.66, ...), kind=kLoop, calls=%fused_computation.6 | loop fusion | flops 74219520 | bytes 5898688 | tf_op jit(solution)/shard_map/reduce_sum | solution.py:82
  115.2 1.0 add_bitcast_fusion
  116.2 7.1 %all-to-all-start = ((f32[1,8,80,384]{3,2,0,1:T(8,128)}), f32[1,8,80,384]{3,2,0,1:T(8,128)S(1)}, u32[]{:S(2)}, u32[]{:S(2)}) async-start(f32[1,8,80,384]{3,2,0,1:T(8,128)} %add_bitcast_fusion), calls=%async_computation | async-start | bytes 1966080 | tf_op jit(solution)/shard_map/all_to_all | solution.py:142
  123.5 4.1 %cosine_multiply_fusion = (f32[640,384]{1,0:T(8,128)S(1)}, f32[640,384]{1,0:T(8,128)S(1)}) fusion(s32[640]{0:T(1024)S(1)} %copy-done.9), kind=kLoop, calls=%fused_computation.47 | loop fusion | flops 2703360 | bytes 1968640 | tf_op jit(solution)/shard_map/mul | solution.py:152
  127.6 12.2 %fusion.14 = f32[2,8,80,1280]{3,2,1,0:T(8,128)S(1)} fusion(f32[2,8,80,384]{3,2,0,1:T(8,128)} %copy-done.2, f32[640,384]{1,0:T(8,128)S(1)} %get-tuple-element.52, f32[640,384]{1,0:T(8,128)S(1)} %get-tuple-element.51), kind=kOutput, calls=%fused_computation.25 | convolution fusion | flops 7550238720 | bytes 10485760 | tf_op jit(solution)/shard_map/fdqn,wn->fdqw/dot_general | solution.py:159
  139.8 1.6 subtract_reduce_fusion
  141.5 9.4 %all-to-all-done = f32[1,8,80,384]{3,2,0,1:T(8,128)S(1)} async-done(((f32[1,8,80,384]{3,2,0,1:T(8,128)}), f32[1,8,80,384]{3,2,0,1:T(8,128)S(1)}, u32[]{:S(2)}, u32[]{:S(2)}) %all-to-all-start) | async-done | bytes 983072 | tf_op jit(solution)/shard_map/all_to_all | solution.py:142
  150.8 5.6 %convolution_bitcast_fusion = f32[1,8,80,1280]{3,2,1,0:T(8,128)S(1)} fusion(f32[640,384]{1,0:T(8,128)S(1)} %get-tuple-element.52, f32[640,384]{1,0:T(8,128)S(1)} %get-tuple-element.51, f32[1,8,80,384]{3,2,0,1:T(8,128)S(1)} %all-to-all-done), kind=kOutput, calls=%fused_computation.20 | convolution fusion | flops 3775365120 | bytes 6225920 | tf_op jit(solution)/shard_map/fdqn,wn->fdqw/dot_general | solution.py:159
  156.4 0.5 subtract_reduce_fusion.1
  157.1 2.3 copy.90
  159.3 2.9 %copy.104 = f32[64,2,10,3,80]{4,3,2,1,0:T(4,128)S(1)} copy(f32[64,2,10,3,80]{4,1,2,0,3:T(2,128)} %bitcast.82) | data formatting | bytes 2457600 | tf_op jit(solution)/shard_map/reshape | solution.py:171
  162.2 2.2 reshape.399
  164.5 45.8 %all_to_all.15 = f32[64,20,240]{2,1,0:T(8,128)S(1)} all-to-all(f32[64,20,240]{2,1,0:T(8,128)} %reshape.399), channel_id=1, replica_groups=mesh['lat'=8,'lon'=8,'lev'=4] {'lat','lon'}, dimensions={0} | all-to-all | bytes 2457600 | tf_op jit(solution)/shard_map/all_to_all | solution.py:173
  210.2 0.4 copy.93
  210.7 2.2 reshape.369
  212.8 2.8 %copy.94 = f32[10,2,3,4,8,2,80]{6,5,4,3,2,1,0:T(2,128)S(1)} copy(f32[10,2,3,4,8,2,80]{6,2,5,3,4,0,1:T(4,128)} %bitcast.80) | data formatting | bytes 2457600 | tf_op jit(solution)/shard_map/transpose | solution.py:179
  215.6 4.3 %reshape.370 = f32[10,24,1280]{2,1,0:T(8,128)} reshape(f32[10,2,3,4,8,2,80]{6,5,4,3,2,1,0:T(2,128)S(1)} %copy.94) | data formatting | bytes 2457600 | tf_op jit(solution)/shard_map/reshape | solution.py:179
  219.9 4.3 %collective-permute-start.2 = (f32[10,24,1280]{2,1,0:T(8,128)}, f32[10,24,1280]{2,1,0:T(8,128)}, u32[]{:S(2)}, u32[]{:S(2)}) collective-permute-start(f32[10,24,1280]{2,1,0:T(8,128)} %reshape.370), channel_id=1, source_target_pairs={{0,1},{1,0},{2,3},{3,2},{4,5},{5,4},{6,7},{7,6},{8,9},{9,8},{10,11... | collective-permute-start | bytes 3686408 | tf_op jit(solution)/shard_map/ppermute | solution.py:185
  224.3 20.4 %collective-permute-done.3 = f32[10,24,1280]{2,1,0:T(8,128)} collective-permute-done((f32[10,24,1280]{2,1,0:T(8,128)}, f32[10,24,1280]{2,1,0:T(8,128)}, u32[]{:S(2)}, u32[]{:S(2)}) %collective-permute-start.3) | collective-permute-done | bytes 1228832 | tf_op jit(solution)/shard_map/ppermute | solution.py:185
  244.6 5.0 %collective-permute-start.4 = (f32[10,24,1280]{2,1,0:T(8,128)}, f32[10,24,1280]{2,1,0:T(8,128)}, u32[]{:S(2)}, u32[]{:S(2)}) collective-permute-start(f32[10,24,1280]{2,1,0:T(8,128)} %collective-permute-done.3), channel_id=1, source_target_pairs={{0,1},{1,0},{2,3},{3,2},{4,5},{5,4},{6,7},{7,6},{8,9},{9,8},{10,11... | collective-permute-start | bytes 3686408 | tf_op jit(solution)/shard_map/ppermute | solution.py:185
  249.8 3.2 %stack_reshape.3 = f32[10,1,24,1280]{3,2,1,0:T(8,128)S(1)} reshape(f32[10,2,3,4,8,2,80]{6,5,4,3,2,1,0:T(2,128)S(1)} %copy.94) | data formatting | bytes 2457600 | tf_op jit(solution)/shard_map/stack;reshape | solution.py:188
  253.1 11.3 %fusion = f32[10,4,24,160]{3,2,1,0:T(8,128)S(1)} fusion(f32[10,160,1280]{2,1,0:T(8,128)} %param.19, f32[10,1,24,1280]{3,2,1,0:T(8,128)} %bitcast.37, f32[10,1,24,1280]{3,2,1,0:T(8,128)} %bitcast.36, f32[10,1,24,1280]{3,2,1,0:T(8,128)} %bitcast.34, f32[10,1,24,1280]{3,2,1,0:T(8,128)S(1)} %stack_reshape.3), kind=kOutput, calls=%fused_computation.2 | convolution fusion | flops 2362982400 | bytes 13721600 | tf_op jit(solution)/shard_map/skqp,snp->skqn/dot_general | solution.py:191
  264.4 0.6 gather_fusion
  265.1 0.6 gather_fusion.1
  266.8 1.1 broadcast_select_fusion
  (72 shorter events, 3.8 us)
Async XLA Ops:
  6.5 78.4 %all-gather.3.cloned.1.call-start = ((), (), s32[]{:S(2)}) async-start(), calls=%async_computation.3 | async-start | bytes 2457600 | tf_op jit(solution)/shard_map/all_gather | solution.py:29
  9.5 29.8 %collective-permute-start.1 = (f32[3,4,160,128]{3,2,1,0:T(8,128)}, f32[3,4,160,128]{3,2,1,0:T(8,128)}, u32[]{:S(2)}, u32[]{:S(2)}) collective-permute-start(f32[3,4,160,128]{3,2,1,0:T(8,128)} %get-tuple-element.37), channel_id=1, source_target_pairs={{4,0},{8,4},{12,8},{16,12},{20,16},{24,20},{28,24},{0,28},{5,1},{9... | collective-permute-start | bytes 2949128 | tf_op jit(solution)/shard_map/ppermute | solution.py:22
  15.9 23.8 %collective-permute-start = (f32[3,4,160,128]{3,2,1,0:T(8,128)}, f32[3,4,160,128]{3,2,1,0:T(8,128)}, u32[]{:S(2)}, u32[]{:S(2)}) collective-permute-start(f32[3,4,160,128]{3,2,1,0:T(8,128)} %get-tuple-element.36), channel_id=1, source_target_pairs={{0,4},{4,8},{8,12},{12,16},{16,20},{20,24},{24,28},{28,0},{1,5},{5... | collective-permute-start | bytes 2949128 | tf_op jit(solution)/shard_map/ppermute | solution.py:19
  23.1 16.6 %copy-start.1 = (f32[3,4,160,384]{3,2,1,0:T(8,128)S(1)}, f32[3,4,160,384]{3,2,1,0:T(8,128)}, u32[]{:S(2)}) copy-start(f32[3,4,160,384]{3,2,1,0:T(8,128)} %param.11) | copy-start | bytes 8847364
  39.3 3.0 %copy-start = (f32[5,384,640]{2,1,0:T(8,128)S(1)}, f32[5,384,640]{2,1,0:T(8,128)}, u32[]{:S(2)}) copy-start(f32[5,384,640]{2,1,0:T(8,128)} %copy.79) | copy-start | bytes 14745604
  42.3 11.9 %copy-start.12 = (s32[160,3]{0,1:T(4,128)S(1)}, s32[160,3]{0,1:T(4,128)}, u32[]{:S(2)}) copy-start(s32[160,3]{0,1:T(4,128)} %param.14) | copy-start | bytes 5764
  51.5 3.7 %copy-start.11 = (f32[32]{0:T(128)S(1)}, f32[32]{0:T(128)}, u32[]{:S(2)}) copy-start(f32[32]{0:T(128)} %param.16) | copy-start | bytes 388
  51.5 3.7 %copy-start.8 = (f32[32]{0:T(128)S(1)}, f32[32]{0:T(128)}, u32[]{:S(2)}) copy-start(f32[32]{0:T(128)} %param.17) | copy-start | bytes 388
  51.5 3.8 %copy-start.10 = (f32[32]{0:T(128)S(1)}, f32[32]{0:T(128)}, u32[]{:S(2)}) copy-start(f32[32]{0:T(128)} %param.15) | copy-start | bytes 388
  55.7 8.1 %copy-start.3 = (f32[1,4,5,32,384]{4,3,1,0,2:T(8,128)S(1)}, f32[1,4,5,32,384]{4,3,1,0,2:T(8,128)}, u32[]{:S(2)}) copy-start(f32[1,4,5,32,384]{4,3,1,0,2:T(8,128)} %get-tuple-element.33) | copy-start | bytes 2949124
  57.3 59.0 %all-to-all-start.1 = ((f32[2,8,80,384]{3,2,0,1:T(8,128)}), f32[2,8,80,384]{3,2,0,1:T(8,128)S(1)}, u32[]{:S(2)}, u32[]{:S(2)}) async-start(f32[2,8,80,384]{3,2,0,1:T(8,128)} %copy.87), calls=%async_computation.1 | async-start | bytes 3932160 | tf_op jit(solution)/shard_map/all_to_all | solution.py:142
  69.4 19.1 %copy-start.6 = (f32[1,4,5,32,384]{4,3,2,1,0:T(8,128)S(1)}, f32[1,4,5,32,384]{4,3,2,1,0:T(8,128)}, u32[]{:S(2)}) copy-start(f32[1,4,5,32,384]{4,3,2,1,0:T(8,128)} %copy.83) | copy-start | bytes 2949124
  85.0 3.6 %copy-start.7 = (f32[1,4,5,32,384]{4,3,2,1,0:T(8,128)S(1)}, f32[1,4,5,32,384]{4,3,2,1,0:T(8,128)}, u32[]{:S(2)}) copy-start(f32[1,4,5,32,384]{4,3,2,1,0:T(8,128)} %copy.82) | copy-start | bytes 2949124
  101.8 13.4 %copy-start.4 = (f32[1,4,5,32,384]{4,3,2,1,0:T(8,128)S(1)}, f32[1,4,5,32,384]{4,3,2,1,0:T(8,128)}, u32[]{:S(2)}) copy-start(f32[1,4,5,32,384]{4,3,2,1,0:T(8,128)} %copy.81) | copy-start | bytes 2949124
  115.0 8.4 %copy-start.9 = (s32[640]{0:T(1024)S(1)}, s32[640]{0:T(1024)}, u32[]{:S(2)}) copy-start(s32[640]{0:T(1024)} %param.18) | copy-start | bytes 7684
  116.2 7.1 %copy-start.2 = (f32[2,8,80,384]{3,2,0,1:T(8,128)}, f32[2,8,80,384]{3,2,0,1:T(8,128)S(1)}, u32[]{:S(2)}) copy-start(f32[2,8,80,384]{3,2,0,1:T(8,128)S(1)} %all-to-all-done.1) | copy-start | bytes 5898244
  116.2 34.6 %all-to-all-start = ((f32[1,8,80,384]{3,2,0,1:T(8,128)}), f32[1,8,80,384]{3,2,0,1:T(8,128)S(1)}, u32[]{:S(2)}, u32[]{:S(2)}) async-start(f32[1,8,80,384]{3,2,0,1:T(8,128)} %add_bitcast_fusion), calls=%async_computation | async-start | bytes 1966080 | tf_op jit(solution)/shard_map/all_to_all | solution.py:142
  150.8 6.1 %copy-start.5 = (f32[2,80,640]{2,1,0:T(8,128)S(1)}, f32[2,80,640]{2,1,0:T(8,128)}, u32[]{:S(2)}) copy-start(f32[2,80,640]{2,1,0:T(8,128)} %get-tuple-element.5) | copy-start | bytes 1228804
  210.2 39.5 %copy-start.14 = (s32[4]{0:T(128)S(1)}, s32[4]{0:T(128)}, u32[]{:S(2)}) copy-start(s32[4]{0:T(128)} %constant.111) | copy-start | bytes 52
  210.2 39.5 %copy-start.13 = (s32[4]{0:T(128)S(1)}, s32[4]{0:T(128)}, u32[]{:S(2)}) copy-start(s32[4]{0:T(128)} %constant.112) | copy-start | bytes 52
  219.9 24.7 %collective-permute-start.3 = (f32[10,24,1280]{2,1,0:T(8,128)}, f32[10,24,1280]{2,1,0:T(8,128)}, u32[]{:S(2)}, u32[]{:S(2)}) collective-permute-start(f32[10,24,1280]{2,1,0:T(8,128)} %reshape.370), channel_id=1, source_target_pairs={{0,2},{1,3},{2,0},{3,1},{4,6},{5,7},{6,4},{7,5},{8,10},{9,11},{10,... | collective-permute-start | bytes 3686408 | tf_op jit(solution)/shard_map/ppermute | solution.py:185
  219.9 33.1 %collective-permute-start.2 = (f32[10,24,1280]{2,1,0:T(8,128)}, f32[10,24,1280]{2,1,0:T(8,128)}, u32[]{:S(2)}, u32[]{:S(2)}) collective-permute-start(f32[10,24,1280]{2,1,0:T(8,128)} %reshape.370), channel_id=1, source_target_pairs={{0,1},{1,0},{2,3},{3,2},{4,5},{5,4},{6,7},{7,6},{8,9},{9,8},{10,11... | collective-permute-start | bytes 3686408 | tf_op jit(solution)/shard_map/ppermute | solution.py:185
  244.6 8.4 %collective-permute-start.4 = (f32[10,24,1280]{2,1,0:T(8,128)}, f32[10,24,1280]{2,1,0:T(8,128)}, u32[]{:S(2)}, u32[]{:S(2)}) collective-permute-start(f32[10,24,1280]{2,1,0:T(8,128)} %collective-permute-done.3), channel_id=1, source_target_pairs={{0,1},{1,0},{2,3},{3,2},{4,5},{5,4},{6,7},{7,6},{8,9},{9,8},{10,11... | collective-permute-start | bytes 3686408 | tf_op jit(solution)/shard_map/ppermute | solution.py:185
Sparse Core Ops, SparseCore 0:
  54.3 30.6 all-gather.2
